TPU v7x, 128 devices: a whole 4x4x4 slice. The times are simulated.
128 devices in a mesh: db: 32 (over z, y, x_hi), section: 2 (over core), mp: 2 (over x_lo).
Axes of the slice: x: 4 (x_hi: 2, x_lo: 2; x = x_hi * 2 + x_lo), y: 4, z: 4, core: 2. Of those that a mesh axis runs over, the one named last changes fastest.
Arguments:
- hidden_in: bfloat16 [16384, 4096], P('db', 'mp'), may hold values from -24 to 24
- database: bfloat16 [128, 128, 896], P('db'), may hold values from -8.5 to 8.5
- neighbour_ids: int32 [256, 2], replicated, may hold values from 0 to 127, as said below
- enc_gain: float32 [896], replicated, may hold values from 0.1 to 1.9
- enc_up: bfloat16 [896, 2048], P(None, ('section', 'mp')), may hold values from -0.1875 to 0.1875
- enc_down: bfloat16 [2048, 896], P(('section', 'mp')), may hold values from -0.125 to 0.125
- dec_gain: float32 [2, 4096], P('section'), may hold values from 0.1 to 1.9
- w_query: bfloat16 [2, 4096, 2048], P('section', None, 'mp'), may hold values from -0.06328125 to 0.06328125
- w_key: bfloat16 [2, 896, 2048], P('section', None, 'mp'), may hold values from -0.135301004 to 0.135301004
- w_value: bfloat16 [2, 896, 2048], P('section', None, 'mp'), may hold values from -0.1875 to 0.1875
- w_out: bfloat16 [2, 2048, 4096], P('section', 'mp'), may hold values from -0.125 to 0.125
Outputs:
- hidden_out: bfloat16 [16384, 4096], P(('db', 'section'), 'mp')
Inputs may be any that keep to these rules, and one draw needn't show every extreme that they name: `neighbour_ids`: block id b is held by db index b // 4. The 16 ids in the rows of one db index name at most 2 blocks of any one holder, and in every draw one holder is named exactly 2 times by every db index.
All inputs are finite; a program needn't handle non-finite values.
Results may differ from a plain program's by a relative error of at most 0.015.
Values may be sent and summed in bfloat16 or wider, within the bound.
No kernel may reach another device: no remote copies, remote signals or barrier semaphores. Data moves between devices by JAX's collectives and lax.ppermute only.
A program may use at most 128 MiB of HBM per device.

v0:
```python
import jax
import jax.numpy as jnp
from jax import lax
from jax.sharding import PartitionSpec as P

HD = 128
E = 896
NEIGH = 2
QBLOCK = 64
NBLOCK = 128


def from_behind(block, axis, distance):
    devices = range(lax.axis_size(axis))
    route = [(i - distance, i) for i in devices if i - distance in devices]
    return lax.ppermute(block, axis, route)


def rms_scale(rows_in, gain_vec):
    return (
        rows_in * lax.rsqrt(jnp.mean(rows_in * rows_in, axis=-1, keepdims=True) + 1e-06) * gain_vec
    )


def encoder_terms(floats, enc_gain, enc_up, enc_down):
    normed = rms_scale(floats, enc_gain).astype(jnp.bfloat16)
    inner_act = jax.nn.gelu(
        jnp.dot(normed, enc_up, preferred_element_type=jnp.float32), approximate=True
    ).astype(jnp.bfloat16)
    return jnp.dot(inner_act, enc_down, preferred_element_type=jnp.float32)


def cross_layer(state_rows, blocks, gain_vec, query_w, key_w, value_w, out_w):
    block_count = blocks.shape[0]
    whole_rows = lax.all_gather(state_rows, "mp", axis=1, tiled=True)
    floats = whole_rows.astype(jnp.float32)
    normed = rms_scale(floats, gain_vec).astype(jnp.bfloat16)
    queries = (jnp.dot(normed, query_w, preferred_element_type=jnp.float32) * HD ** (-0.5)).astype(
        jnp.bfloat16
    )
    flat_rows = blocks.reshape(-1, E)
    key_rows = jnp.dot(flat_rows, key_w, preferred_element_type=jnp.float32).astype(jnp.bfloat16)
    value_rows = jnp.dot(flat_rows, value_w, preferred_element_type=jnp.float32).astype(
        jnp.bfloat16
    )
    head_count = query_w.shape[1] // HD
    query_four = queries.reshape(block_count, QBLOCK, head_count, HD)
    key_four = key_rows.reshape(block_count, NEIGH * NBLOCK, head_count, HD)
    value_four = value_rows.reshape(block_count, NEIGH * NBLOCK, head_count, HD)
    scores = jnp.einsum("cqhd,ckhd->chqk", query_four, key_four, preferred_element_type=jnp.float32)
    soft_weights = jax.nn.softmax(scores, axis=-1).astype(jnp.bfloat16)
    context = jnp.einsum(
        "chqk,ckhd->cqhd", soft_weights, value_four, preferred_element_type=jnp.float32
    )
    context = context.astype(jnp.bfloat16).reshape(block_count * QBLOCK, head_count * HD)
    partial_out = jnp.dot(context, out_w, preferred_element_type=jnp.float32)
    head_share = lax.psum_scatter(partial_out, "mp", scatter_dimension=1, tiled=True)
    return (state_rows.astype(jnp.float32) + head_share).astype(jnp.bfloat16)


def body(
    hidden_in,
    database,
    neighbour_ids,
    enc_gain,
    enc_up,
    enc_down,
    dec_gain,
    w_query,
    w_key,
    w_value,
    w_out,
):
    db_count = lax.axis_size("db")
    db_index = lax.axis_index("db")
    blocks_held = database.shape[0]
    request = neighbour_ids.shape[0] // db_count * NEIGH
    capacity = max(2, (request + db_count - 1) // db_count)
    id_table = neighbour_ids.reshape(db_count, request)
    owners = id_table // blocks_held
    within = id_table % blocks_held
    places = jnp.arange(request)
    same_owner = owners[:, :, None] == owners[:, None, :]
    earlier = places[None, :, None] > places[None, None, :]
    rank_in = jnp.sum((same_owner & earlier).astype(jnp.int32), axis=-1)
    slot_ids = jnp.arange(capacity)
    matches = (owners[:, None, :] == db_index) & (rank_in[:, None, :] == slot_ids[None, :, None])
    send_local = jnp.sum(matches.astype(jnp.int32) * within[:, None, :], axis=-1)
    my_owner = lax.dynamic_index_in_dim(owners, db_index, 0, keepdims=False)
    my_rank = lax.dynamic_index_in_dim(rank_in, db_index, 0, keepdims=False)
    slot_pick = my_owner * capacity + my_rank
    payload = database[send_local]
    received = lax.all_to_all(payload, "db", split_axis=0, concat_axis=0, tiled=True)
    fetched = received.reshape(db_count * capacity, NBLOCK, E)[slot_pick]
    fetched_floats = fetched.reshape(-1, E).astype(jnp.float32)
    fetched_terms = lax.psum(
        encoder_terms(fetched_floats, enc_gain, enc_up, enc_down), ("section", "mp")
    )
    encoded = (fetched_floats + fetched_terms).astype(jnp.bfloat16)
    query_blocks = request // NEIGH
    enc_blocks = encoded.reshape(query_blocks, NEIGH * NBLOCK, E)
    segments = lax.axis_size("section")
    segment_index = lax.axis_index("section")
    micro_tokens = hidden_in.shape[0] // segments
    micro_blocks = micro_tokens // QBLOCK
    arrived = jnp.zeros((micro_tokens, hidden_in.shape[1]), jnp.bfloat16)
    finished = []
    for turn_id in range(2 * segments - 1):
        start_row = min(turn_id, segments - 1) * micro_tokens
        entering = hidden_in[start_row : start_row + micro_tokens]
        current = jnp.where(segment_index == 0, entering, arrived)
        micro_pick = jnp.clip(turn_id - segment_index, 0, segments - 1)
        neighbours = lax.dynamic_slice_in_dim(
            enc_blocks, micro_pick * micro_blocks, micro_blocks, 0
        )
        leaving = cross_layer(
            current, neighbours, dec_gain[0], w_query[0], w_key[0], w_value[0], w_out[0]
        )
        if turn_id >= segments - 1:
            finished.append(leaving)
        if turn_id < 2 * segments - 2:
            arrived = from_behind(leaving, "section", 1)
    result = finished[segments - 1]
    moved_rows = from_behind(finished[0], "section", 0 - (segments - 1))
    result = jnp.where(segment_index == 0, moved_rows, result)
    return result


def solution(mesh):
    in_specs = (
        P("db", "mp"),
        P("db", None, None),
        P(),
        P(),
        P(None, ("section", "mp")),
        P(("section", "mp"), None),
        P("section", None),
        P("section", None, "mp"),
        P("section", None, "mp"),
        P("section", None, "mp"),
        P("section", "mp", None),
    )
    out_specs = P(("db", "section"), "mp")
    return jax.shard_map(body, mesh=mesh, in_specs=in_specs, out_specs=out_specs, check_vma=False)
```

profile of v0, /device:TPU:1, one launch (start us, length us, event | category | flops | bytes accessed | tf_op | source)
XLA Modules:
  0.0 919.1 jit_solution(2563800234305476005)
XLA Ops:
  7.4 0.9 copy.54
  8.9 9.0 gather_fusion
  17.9 11.6 %all-to-all-start = ((bf16[32,2,128,896]{3,2,1,0:T(8,128)(2,1)}), bf16[32,2,128,896]{3,2,1,0:T(8,128)(2,1)}, u32[]{:S(2)}, u32[]{:S(2)}) async-start(bf16[32,2,128,896]{3,2,1,0:T(8,128)(2,1)} %bitcast.144), calls=%async_computation | async-start | bytes 29360128 | tf_op jit(solution)/shard_map/all_to_all | solution.py:93
  29.6 2.3 slice_select_fusion
  32.1 206.9 %all-to-all-done = bf16[32,2,128,896]{3,2,1,0:T(8,128)(2,1)} async-done(((bf16[32,2,128,896]{3,2,1,0:T(8,128)(2,1)}), bf16[32,2,128,896]{3,2,1,0:T(8,128)(2,1)}, u32[]{:S(2)}, u32[]{:S(2)}) %all-to-all-start) | async-done | bytes 14680096 | tf_op jit(solution)/shard_map/all_to_all | solution.py:93
  239.1 7.9 gather_fusion.1
  247.0 3.0 fusion.15
  250.1 2.7 fusion.17
  252.8 10.5 %fusion.36 = f32[2048,896]{1,0:T(8,128)} fusion(bf16[512,896]{1,0:T(8,128)(2,1)S(1)} %copy-done.21, bf16[2048,896]{1,0:T(8,128)(2,1)} %fusion.17, bf16[896,512]{1,0:T(8,128)(2,1)} %param.15), kind=kOutput, calls=%fused_computation.48 | convolution fusion | flops 3767533568 | bytes 12845056 | tf_op jit(solution)/shard_map/dot_general | solution.py:30
  263.6 2.2 fusion.19
  265.9 5.8 fusion.108
  271.8 290.7 %all-reduce.2.cloned.1.call-done = f32[2048,896]{1,0:T(8,128)} async-done(((f32[2048,896]{1,0:T(8,128)}), f32[2048,896]{1,0:T(8,128)}) %all-reduce.2.cloned.1.call-update) | async-done | bytes 7340048 | tf_op jit(solution)/shard_map/psum | solution.py:96
  562.4 4.8 fusion.18
  567.2 2.3 constant_dynamic-slice_fusion.2
  569.6 2.3 convert_bitcast_fusion.4
  572.0 0.6 copy.73
  572.6 0.9 fusion.51
  573.4 1.3 copy-done.8
  574.7 0.6 fusion.156
  575.4 0.9 copy-done.18
  576.2 2.3 convert_bitcast_fusion.5
  578.6 2.0 copy.74
  580.6 6.5 fusion.129
  587.4 7.6 fusion.7
  595.2 58.0 %reduce-scatter.4.cloned.1.call-done = f32[256,2048]{1,0:T(8,128)} async-done(((f32[256,4096]{1,0:T(8,128)}), f32[256,2048]{1,0:T(8,128)}) %reduce-scatter.4.cloned.1.call-update) | async-done | bytes 2097168 | tf_op jit(solution)/shard_map/reduce_scatter | solution.py:57
  653.2 2.3 add_convert_fusion.2
  655.5 1.3 collective-permute-start
  656.8 3.3 collective-permute-done
  660.1 1.1 broadcast_select_fusion.1
  661.6 3.8 convert_bitcast_fusion.2
  665.5 2.0 copy.77
  667.5 0.8 copy-done.19
  668.3 2.3 convert_bitcast_fusion.3
  670.6 1.9 copy.78
  672.5 24.7 %all-gather.6.cloned.1.call-done = bf16[256,4096]{1,0:T(8,128)(2,1)} async-done(((bf16[256,2048]{1,0:T(8,128)(2,1)}), bf16[256,4096]{1,0:T(8,128)(2,1)}) %all-gather.6.cloned.1.call-update) | async-done | bytes 2097168 | tf_op jit(solution)/shard_map/all_gather | solution.py:35
  697.2 2.2 fusion.22
  699.5 5.9 fusion.113
  705.5 0.8 fusion.47
  706.4 1.3 copy-done.9
  707.7 0.6 fusion.157
  708.4 6.5 fusion.126
  715.2 7.6 fusion.5
  723.0 58.0 %reduce-scatter.6.cloned.1.call-done = f32[256,2048]{1,0:T(8,128)} async-done(((f32[256,4096]{1,0:T(8,128)}), f32[256,2048]{1,0:T(8,128)}) %reduce-scatter.6.cloned.1.call-update) | async-done | bytes 2097168 | tf_op jit(solution)/shard_map/reduce_scatter | solution.py:57
  780.9 2.0 add_convert_fusion.1
  783.0 1.3 collective-permute-start.2
  784.3 3.3 collective-permute-done.2
  787.5 1.2 broadcast_select_fusion
  788.9 3.8 convert_bitcast_fusion
  792.8 2.0 copy.81
  794.8 0.8 copy-done.20
  795.6 2.3 convert_bitcast_fusion.1
  797.9 1.9 copy.82
  799.9 24.9 %all-gather.8.cloned.1.call-done = bf16[256,4096]{1,0:T(8,128)(2,1)} async-done(((bf16[256,2048]{1,0:T(8,128)(2,1)}), bf16[256,4096]{1,0:T(8,128)(2,1)}) %all-gather.8.cloned.1.call-update) | async-done | bytes 2097168 | tf_op jit(solution)/shard_map/all_gather | solution.py:35
  824.8 2.2 fusion.25
  827.0 5.9 fusion.118
  833.1 0.8 fusion.43
  833.9 1.3 copy-done.10
  835.3 0.6 fusion.158
  835.9 6.5 fusion.123
  842.8 7.6 fusion.3
  850.5 3.9 collective-permute-start.1
  854.4 1.6 collective-permute-done.1
  856.0 52.5 %reduce-scatter.8.cloned.1.call-done = f32[256,2048]{1,0:T(8,128)} async-done(((f32[256,4096]{1,0:T(8,128)}), f32[256,2048]{1,0:T(8,128)}) %reduce-scatter.8.cloned.1.call-update) | async-done | bytes 2097168 | tf_op jit(solution)/shard_map/reduce_scatter | solution.py:57
  908.5 3.0 fusion.132
  (79 shorter events, 3.5 us)
Async XLA Ops:
  7.4 562.2 %copy-start = (bf16[1,896,1024]{2,1,0:T(8,128)(2,1)S(1)}, bf16[1,896,1024]{2,1,0:T(8,128)(2,1)}, u32[]{:S(2)}) copy-start(bf16[1,896,1024]{2,1,0:T(8,128)(2,1)} %param.19) | copy-start | bytes 5505028
  17.9 221.2 %all-to-all-start = ((bf16[32,2,128,896]{3,2,1,0:T(8,128)(2,1)}), bf16[32,2,128,896]{3,2,1,0:T(8,128)(2,1)}, u32[]{:S(2)}, u32[]{:S(2)}) async-start(bf16[32,2,128,896]{3,2,1,0:T(8,128)(2,1)} %bitcast.144), calls=%async_computation | async-start | bytes 29360128 | tf_op jit(solution)/shard_map/all_to_all | solution.py:93
  29.5 234.1 %all-gather.4.cloned.1.call-start = ((), (), s32[]{:S(2)}) async-start(), calls=%async_computation.5 | async-start | bytes 3145728 | tf_op jit(solution)/shard_map/all_gather | solution.py:35
  31.8 530.6 %all-reduce.2.cloned.1.call-start = ((), (), s32[]{:S(2)}) async-start(), calls=%async_computation.4 | async-start | bytes 14680064 | tf_op jit(solution)/shard_map/psum | solution.py:96
  247.0 3.1 copy-start.1
  247.0 3.1 copy-start.17
  250.1 2.7 copy-start.21
  263.3 2.5 copy-start.22
  263.3 389.8 %reduce-scatter.4.cloned.1.call-start = ((), (), s32[]{:S(2)}) async-start(), calls=%async_computation.6 | async-start | bytes 6291456 | tf_op jit(solution)/shard_map/reduce_scatter | solution.py:57
  263.6 2.3 copy-start.11
  573.4 1.3 copy-start.8
  574.7 1.5 copy-start.18
  595.1 102.1 %all-gather.6.cloned.1.call-start = ((), (), s32[]{:S(2)}) async-start(), calls=%async_computation.7 | async-start | bytes 3145728 | tf_op jit(solution)/shard_map/all_gather | solution.py:35
  653.2 6.9 copy-start.4
  655.5 4.6 collective-permute-start
  661.2 119.7 %reduce-scatter.6.cloned.1.call-start = ((), (), s32[]{:S(2)}) async-start(), calls=%async_computation.8 | async-start | bytes 6291456 | tf_op jit(solution)/shard_map/reduce_scatter | solution.py:57
  665.5 2.0 copy-start.15
  665.5 2.8 copy-start.19
  697.2 2.2 copy-start.13
  699.5 6.0 copy-start.6
  706.4 1.4 copy-start.9
  722.9 58.0 %copy-start.3 = (bf16[256,2048]{1,0:T(8,128)(2,1)S(1)}, bf16[256,2048]{1,0:T(8,128)(2,1)}, u32[]{:S(2)}) copy-start(bf16[256,2048]{1,0:T(8,128)(2,1)} %broadcast_select_fusion.1) | copy-start | bytes 3145732
  722.9 101.9 %all-gather.8.cloned.1.call-start = ((), (), s32[]{:S(2)}) async-start(), calls=%async_computation.9 | async-start | bytes 3145728 | tf_op jit(solution)/shard_map/all_gather | solution.py:35
  780.9 6.6 copy-start.5
  782.9 4.6 copy-start.16
  783.0 4.6 collective-permute-start.2
  788.7 119.7 %reduce-scatter.8.cloned.1.call-start = ((), (), s32[]{:S(2)}) async-start(), calls=%async_computation.10 | async-start | bytes 6291456 | tf_op jit(solution)/shard_map/reduce_scatter | solution.py:57
  792.8 2.0 copy-start.14
  792.8 2.8 copy-start.20
  824.8 2.2 copy-start.12
  827.0 6.0 copy-start.7
  833.9 1.4 copy-start.10
  850.4 58.0 %copy-start.2 = (bf16[256,2048]{1,0:T(8,128)(2,1)S(1)}, bf16[256,2048]{1,0:T(8,128)(2,1)}, u32[]{:S(2)}) copy-start(bf16[256,2048]{1,0:T(8,128)(2,1)} %broadcast_select_fusion) | copy-start | bytes 3145732
  850.5 5.5 collective-permute-start.1
Sparse Core Ops, SparseCore 0:
  32.0 59.7 all-gather.3
  595.2 57.8 reduce-scatter.3
  661.3 35.8 all-gather.5
  723.0 57.8 reduce-scatter.5
  788.8 35.8 all-gather.7
  850.6 57.8 reduce-scatter.7
Sparse Core Ops, SparseCore 1:
  263.4 298.9 all-reduce.1
where the time goes:
time: 927 us; the launch traced here: 919 us
  waiting for transfers between devices  724 us (78%)
  matrix products  90.1 us (10%)
  local copies, waits for them, and re-layouts  39 us (4%)
  other arithmetic  31.4 us (3%)
  starting transfers between devices  19.1 us (2%)
  between operations  15.6 us (2%)
    psum x1, waiting for transfers between devices, body(): lax.psum(encoder_terms(fetched_floats, enc_gain, enc_up, enc_down), ('sec...  291 us
    all_to_all x1, waiting for transfers between devices, body(): lax.all_to_all(payload, 'db', split_axis=0, concat_axis=0, tiled=True)  207 us
    reduce_scatter x3, waiting for transfers between devices, cross_layer(): lax.psum_scatter(partial_out, 'mp', scatter_dimension=1, tiled=True)  168 us
    all_gather x3, waiting for transfers between devices, cross_layer(): whole_rows = lax.all_gather(state_rows, 'mp', axis=1, tiled=True)  49.6 us
    dot_general x3, matrix products, cross_layer(): partial_out = jnp.dot(context, out_w, preferred_element_type=jnp.float32)  22.9 us
    dot_general x3, matrix products, cross_layer(): jnp.einsum('chqk,ckhd->cqhd', soft_weights, value_four, preferred_element...  19.5 us
  transfers between devices with their start and end apart: 11, of which 10 were waited for; matrix products, arithmetic and copies ran while one was open for 6% of the time, Pallas kernels for 0%

commit v1 on v0

--- a/solution.py
+++ b/solution.py
@@ -8,12 +8,6 @@
 NEIGH = 2
 QBLOCK = 64
 NBLOCK = 128
-
-
-def from_behind(block, axis, distance):
-    devices = range(lax.axis_size(axis))
-    route = [(i - distance, i) for i in devices if i - distance in devices]
-    return lax.ppermute(block, axis, route)
 
 
 def rms_scale(rows_in, gain_vec):
@@ -73,57 +67,71 @@
 ):
     db_count = lax.axis_size("db")
     db_index = lax.axis_index("db")
+    channels = lax.axis_size("section")
+    sec_index = lax.axis_index("section")
+    halves = lax.axis_size("mp")
+    mp_index = lax.axis_index("mp")
     blocks_held = database.shape[0]
     request = neighbour_ids.shape[0] // db_count * NEIGH
-    capacity = max(2, (request + db_count - 1) // db_count)
+    per_channel = request // channels
+    half_rows = NBLOCK // halves
+    quarter = half_rows // channels
+
+    held_rows = database.reshape(-1, E).astype(jnp.float32)
+    terms = lax.psum(encoder_terms(held_rows, enc_gain, enc_up, enc_down), "section")
+    terms = terms.reshape(blocks_held, halves, channels, quarter, E)
+    terms = lax.dynamic_index_in_dim(terms, sec_index, 2, keepdims=False)
+    terms = lax.psum_scatter(terms, "mp", scatter_dimension=1, tiled=True)
+    terms = lax.all_gather(terms, "section", axis=2, tiled=True)
+    terms = terms.reshape(blocks_held, half_rows, E)
+    own_rows = lax.dynamic_slice_in_dim(database, mp_index * half_rows, half_rows, 1)
+    enc_half = (own_rows.astype(jnp.float32) + terms).astype(jnp.bfloat16)
+
     id_table = neighbour_ids.reshape(db_count, request)
     owners = id_table // blocks_held
     within = id_table % blocks_held
     places = jnp.arange(request)
     same_owner = owners[:, :, None] == owners[:, None, :]
-    earlier = places[None, :, None] > places[None, None, :]
+    earlier = places[None, None, :] < places[None, :, None]
     rank_in = jnp.sum((same_owner & earlier).astype(jnp.int32), axis=-1)
-    slot_ids = jnp.arange(capacity)
-    matches = (owners[:, None, :] == db_index) & (rank_in[:, None, :] == slot_ids[None, :, None])
-    send_local = jnp.sum(matches.astype(jnp.int32) * within[:, None, :], axis=-1)
+    single = jnp.sum(same_owner.astype(jnp.int32), axis=-1) == 1
+    singles_before = jnp.sum((single[:, None, :] & earlier).astype(jnp.int32), axis=-1)
+    channel = jnp.where(single, singles_before % channels, rank_in)
+    same_channel = channel[:, :, None] == channel[:, None, :]
+    slot_in = jnp.sum((same_channel & earlier).astype(jnp.int32), axis=-1)
+
+    serve = (owners == db_index) & (channel == sec_index)
+    send_local = jnp.sum(jnp.where(serve, within, 0), axis=-1)
+    payload = enc_half[send_local]
+    received = lax.all_to_all(payload, "db", split_axis=0, concat_axis=0, tiled=True)
+
     my_owner = lax.dynamic_index_in_dim(owners, db_index, 0, keepdims=False)
-    my_rank = lax.dynamic_index_in_dim(rank_in, db_index, 0, keepdims=False)
-    slot_pick = my_owner * capacity + my_rank
-    payload = database[send_local]
-    received = lax.all_to_all(payload, "db", split_axis=0, concat_axis=0, tiled=True)
-    fetched = received.reshape(db_count * capacity, NBLOCK, E)[slot_pick]
-    fetched_floats = fetched.reshape(-1, E).astype(jnp.float32)
-    fetched_terms = lax.psum(
-        encoder_terms(fetched_floats, enc_gain, enc_up, enc_down), ("section", "mp")
+    my_channel = lax.dynamic_index_in_dim(channel, db_index, 0, keepdims=False)
+    my_slot = lax.dynamic_index_in_dim(slot_in, db_index, 0, keepdims=False)
+    pick = (my_channel[None, :] == sec_index) & (
+        my_slot[None, :] == jnp.arange(per_channel)[:, None]
     )
-    encoded = (fetched_floats + fetched_terms).astype(jnp.bfloat16)
-    query_blocks = request // NEIGH
-    enc_blocks = encoded.reshape(query_blocks, NEIGH * NBLOCK, E)
-    segments = lax.axis_size("section")
-    segment_index = lax.axis_index("section")
-    micro_tokens = hidden_in.shape[0] // segments
-    micro_blocks = micro_tokens // QBLOCK
-    arrived = jnp.zeros((micro_tokens, hidden_in.shape[1]), jnp.bfloat16)
-    finished = []
-    for turn_id in range(2 * segments - 1):
-        start_row = min(turn_id, segments - 1) * micro_tokens
-        entering = hidden_in[start_row : start_row + micro_tokens]
-        current = jnp.where(segment_index == 0, entering, arrived)
-        micro_pick = jnp.clip(turn_id - segment_index, 0, segments - 1)
-        neighbours = lax.dynamic_slice_in_dim(
-            enc_blocks, micro_pick * micro_blocks, micro_blocks, 0
+    slot_owner = jnp.sum(jnp.where(pick, my_owner[None, :], 0), axis=-1)
+    compact = received[slot_owner]
+    channel_blocks = lax.all_gather(compact, "mp", axis=1, tiled=True)
+    all_blocks = lax.all_gather(channel_blocks, "section", axis=0, tiled=True)
+    flat_pos = my_channel * per_channel + my_slot
+    mine = lax.dynamic_slice_in_dim(flat_pos, sec_index * per_channel, per_channel, 0)
+    neighbours = all_blocks[mine]
+    enc_blocks = neighbours.reshape(-1, NEIGH * NBLOCK, E)
+
+    micro_tokens = hidden_in.shape[0] // channels
+    state = lax.dynamic_slice_in_dim(hidden_in, sec_index * micro_tokens, micro_tokens, 0)
+    gains = lax.all_gather(dec_gain, "section", axis=0, tiled=True)
+    wq = lax.all_gather(w_query, "section", axis=0, tiled=True)
+    wk = lax.all_gather(w_key, "section", axis=0, tiled=True)
+    wv = lax.all_gather(w_value, "section", axis=0, tiled=True)
+    wo = lax.all_gather(w_out, "section", axis=0, tiled=True)
+    for layer_id in range(wq.shape[0]):
+        state = cross_layer(
+            state, enc_blocks, gains[layer_id], wq[layer_id], wk[layer_id], wv[layer_id], wo[layer_id]
         )
-        leaving = cross_layer(
-            current, neighbours, dec_gain[0], w_query[0], w_key[0], w_value[0], w_out[0]
-        )
-        if turn_id >= segments - 1:
-            finished.append(leaving)
-        if turn_id < 2 * segments - 2:
-            arrived = from_behind(leaving, "section", 1)
-    result = finished[segments - 1]
-    moved_rows = from_behind(finished[0], "section", 0 - (segments - 1))
-    result = jnp.where(segment_index == 0, moved_rows, result)
-    return result
+    return state
 
 
 def solution(mesh):

time: 927 us -> 535 us (0.58)
  waiting for transfers between devices: 724 us -> 404 us
  matrix products: 90.1 us -> 59.7 us
  other arithmetic: 31.4 us -> 15.8 us
  local copies, waits for them, and re-layouts: 39 us -> 25.4 us
    psum x1, waiting for transfers between devices: 291 us -> 30.1 us  [body(): lax.psum(encoder_terms(held_rows, enc_gain, enc_up, enc_down), 'section')]
    all_to_all x1, waiting for transfers between devices: 207 us -> 47.8 us  [body(): lax.all_to_all(payload, 'db', split_axis=0, concat_axis=0, tiled=True)]
    all_gather x0 -> x6, waiting for transfers between devices: none -> 128 us  [the longest x1 34.2 us: body(): channel_blocks = lax.all_gather(compact, 'mp', axis=1, tiled=True)]
    reduce_scatter x3 -> x2, waiting for transfers between devices: 168 us -> 116 us  [cross_layer(): lax.psum_scatter(partial_out, 'mp', scatter_dimension=1, tiled=True)]
    reduce_scatter x0 -> x1, waiting for transfers between devices: none -> 20.5 us  [body(): terms = lax.psum_scatter(terms, 'mp', scatter_dimension=1, tiled=True)]
    all_gather x3 -> x2, waiting for transfers between devices: 49.6 us -> 58.7 us  [cross_layer(): whole_rows = lax.all_gather(state_rows, 'mp', axis=1, tiled=True)]
    dot_general x3 -> x2, matrix products: 22.9 us -> 15.4 us  [cross_layer(): partial_out = jnp.dot(context, out_w, preferred_element_type=jnp.float32)]
    dot_general x3 -> x2, matrix products: 19.5 us -> 12.7 us  [cross_layer(): jnp.einsum('chqk,ckhd->cqhd', soft_weights, value_four, preferred_element...]
  transfers between devices with their start and end apart: 11 -> 13, of which waited for: 10 -> 13; matrix products, arithmetic and copies ran while one was open for 6% -> 8% of each run, Pallas kernels for 0% -> 0%
where the time goes in v1:
time: 535 us; the launch traced here: 534 us
  waiting for transfers between devices  404 us (76%)
  matrix products  59.7 us (11%)
  local copies, waits for them, and re-layouts  25.4 us (5%)
  other arithmetic  15.8 us (3%)
  between operations  14 us (3%)
  starting transfers between devices  9.86 us (2%)
  blocking collectives  5.63 us (1%)
    reduce_scatter x2, waiting for transfers between devices, cross_layer(): lax.psum_scatter(partial_out, 'mp', scatter_dimension=1, tiled=True)  116 us
    all_gather x2, waiting for transfers between devices, cross_layer(): whole_rows = lax.all_gather(state_rows, 'mp', axis=1, tiled=True)  58.7 us
    all_to_all x1, waiting for transfers between devices, body(): lax.all_to_all(payload, 'db', split_axis=0, concat_axis=0, tiled=True)  47.8 us
    all_gather x1, waiting for transfers between devices, body(): channel_blocks = lax.all_gather(compact, 'mp', axis=1, tiled=True)  34.2 us
    psum x1, waiting for transfers between devices, body(): lax.psum(encoder_terms(held_rows, enc_gain, enc_up, enc_down), 'section')  30.1 us
    all_gather x1, waiting for transfers between devices, body(): wq = lax.all_gather(w_query, 'section', axis=0, tiled=True)  29.5 us
    reduce_scatter x1, waiting for transfers between devices, body(): terms = lax.psum_scatter(terms, 'mp', scatter_dimension=1, tiled=True)  20.5 us
    all_gather x1, waiting for transfers between devices, body(): wo = lax.all_gather(w_out, 'section', axis=0, tiled=True)  18.3 us
  transfers between devices with their start and end apart: 13, of which 13 were waited for; matrix products, arithmetic and copies ran while one was open for 8% of the time, Pallas kernels for 0%

profile of v1, /device:TPU:1, one launch (start us, length us, event | category | flops | bytes accessed | tf_op | source)
XLA Modules:
  0.0 534.3 jit_solution(12195174824502287103)
XLA Ops:
  6.5 1.6 multiply_reduce_fusion
  8.1 1.5 fusion.27
  9.6 2.6 fusion.69
  12.3 30.1 %all-reduce.2.cloned.1.call-done = f32[4,2,2,32,896]{4,3,2,1,0:T(8,128)} async-done(((f32[4,2,2,32,896]{4,3,2,1,0:T(8,128)}), f32[4,2,2,32,896]{4,3,2,1,0:T(8,128)}) %all-reduce.2.cloned.1.call-update) | async-done | bytes 1835024 | tf_op jit(solution)/shard_map/psum | solution.py:81
  42.4 2.2 copy_bitcast_fusion
  44.6 0.1 copy.78
  44.8 0.2 copy.83
  46.0 0.3 fusion.87
  46.5 20.5 %reduce-scatter.4.cloned.1.call-done = f32[4,1,32,896]{3,2,0,1:T(8,128)} async-done(((f32[4,2,32,896]{3,2,0,1:T(8,128)}), f32[4,1,32,896]{3,2,0,1:T(8,128)}) %reduce-scatter.4.cloned.1.call-update) | async-done | bytes 458768 | tf_op jit(solution)/shard_map/reduce_scatter | solution.py:84
  67.0 3.1 all_gather.30
  70.3 2.8 gather_fusion
  73.1 9.2 %all-to-all-start = ((bf16[32,64,896]{2,1,0:T(8,128)(2,1)}), bf16[32,64,896]{2,1,0:T(8,128)(2,1)}, u32[]{:S(2)}, u32[]{:S(2)}) async-start(bf16[32,64,896]{2,1,0:T(8,128)(2,1)} %gather_fusion), calls=%async_computation.1 | async-start | bytes 7340032 | tf_op jit(solution)/shard_map/all_to_all | solution.py:106
  82.5 0.2 dynamic-slice_reduce_fusion.1
  82.6 0.2 compare_reduce_fusion
  82.8 0.2 multiply_reduce_fusion.1
  83.2 47.8 %all-to-all-done = bf16[32,64,896]{2,1,0:T(8,128)(2,1)} async-done(((bf16[32,64,896]{2,1,0:T(8,128)(2,1)}), bf16[32,64,896]{2,1,0:T(8,128)(2,1)}, u32[]{:S(2)}, u32[]{:S(2)}) %all-to-all-start) | async-done | bytes 3670048 | tf_op jit(solution)/shard_map/all_to_all | solution.py:106
  131.0 3.6 gather_fusion.1
  134.7 1.0 constant_dynamic-slice_fusion.1
  135.8 34.2 %all-gather.24.cloned.1.call-done = bf16[8,128,896]{2,1,0:T(8,128)(2,1)} async-done(((bf16[8,64,896]{2,1,0:T(8,128)(2,1)}), bf16[8,128,896]{2,1,0:T(8,128)(2,1)}) %all-gather.24.cloned.1.call-update) | async-done | bytes 1835024 | tf_op jit(solution)/shard_map/all_gather | solution.py:116
  170.1 0.5 all-gather.18.cloned.1.call-update
  170.6 0.7 all-gather.12.cloned.1.call-update
  171.4 0.7 all-gather.16.cloned.1.call-update
  172.1 0.7 all-gather.20.cloned.1.call-update
  172.9 2.5 all-gather.2
  175.5 32.6 %all-gather.14.cloned.1.call-done = bf16[256,4096]{1,0:T(8,128)(2,1)} async-done(((bf16[256,2048]{1,0:T(8,128)(2,1)}), bf16[256,4096]{1,0:T(8,128)(2,1)}) %all-gather.14.cloned.1.call-update) | async-done | bytes 2097168 | tf_op jit(solution)/shard_map/all_gather | solution.py:29
  208.1 2.1 fusion.6
  210.2 16.6 %all-gather.26.cloned.1.call-done = bf16[16,128,896]{2,1,0:T(8,128)(2,1)} async-done(((bf16[8,128,896]{2,1,0:T(8,128)(2,1)}), bf16[16,128,896]{2,1,0:T(8,128)(2,1)}) %all-gather.26.cloned.1.call-update) | async-done | bytes 3670032 | tf_op jit(solution)/shard_map/all_gather | solution.py:117
  226.8 2.9 gather_fusion.2
  229.7 15.6 %all-gather.18.cloned.1.call-done = bf16[2,896,1024]{2,1,0:T(8,128)(2,1)} async-done(((bf16[1,896,1024]{2,1,0:T(8,128)(2,1)}), bf16[2,896,1024]{2,1,0:T(8,128)(2,1)}) %all-gather.18.cloned.1.call-update) | async-done | bytes 3670032 | tf_op jit(solution)/shard_map/all_gather | solution.py:127
  245.3 3.8 convert_bitcast_fusion.2
  249.1 0.6 copy.120
  249.7 14.2 %all-gather.12.cloned.1.call-done = bf16[2,896,1024]{2,1,0:T(8,128)(2,1)} async-done(((bf16[1,896,1024]{2,1,0:T(8,128)(2,1)}), bf16[2,896,1024]{2,1,0:T(8,128)(2,1)}) %all-gather.12.cloned.1.call-update) | async-done | bytes 3670032 | tf_op jit(solution)/shard_map/all_gather | solution.py:128
  263.9 4.4 convert_bitcast_fusion.3
  268.3 1.9 copy.121
  270.2 29.5 %all-gather.16.cloned.1.call-done = bf16[2,4096,1024]{2,1,0:T(8,128)(2,1)} async-done(((bf16[1,4096,1024]{2,1,0:T(8,128)(2,1)}), bf16[2,4096,1024]{2,1,0:T(8,128)(2,1)}) %all-gather.16.cloned.1.call-update) | async-done | bytes 16777232 | tf_op jit(solution)/shard_map/all_gather | solution.py:126
  299.7 6.4 %fusion.52 = bf16[32,8,8,128]{3,1,2,0:T(8,128)(2,1)S(1)} fusion(bf16[2,4096,1024]{2,1,0:T(8,128)(2,1)} %all-gather.16.cloned.1.call-done, bf16[256,4096]{1,0:T(8,128)(2,1)} %all-gather.14.cloned.1.call-done, f32[4096]{0:T(1024)S(1)} %bitcast.127, f32[256]{0:T(256)S(1)} %add_rsqrt_fusion.1), kind=kOutput, calls=%fused_computation.62 | convolution fusion | flops 2152202240 | bytes 11027456 | tf_op jit(solution)/shard_map/dot_general | solution.py:32
  306.2 0.8 fusion.20
  307.1 1.4 copy-done.3
  308.4 0.6 fusion.104
  309.1 1.0 copy-done.10
  310.0 6.8 %fusion.49 = bf16[4,64,8,128]{3,1,2,0:T(8,128)(2,1)S(1)} fusion(bf16[4,256,8,128]{3,2,1,0:T(8,128)(2,1)S(1)} %bitcast.117, f32[4,8,64]{2,1,0:T(8,128)S(1)} %fusion.104, f32[4,8,64,256]{3,2,1,0:T(8,128)} %copy-done.3), kind=kOutput, calls=%fused_computation.61 | convolution fusion | flops 136055040 | bytes 4726784 | tf_op jit(solution)/shard_map/chqk,ckhd->cqhd/dot_general | solution.py:46
  316.8 0.3 copy.96
  317.2 18.3 %all-gather.20.cloned.1.call-done = bf16[2,1024,4096]{2,1,0:T(8,128)(2,1)} async-done(((bf16[1,1024,4096]{2,1,0:T(8,128)(2,1)}), bf16[2,1024,4096]{2,1,0:T(8,128)(2,1)}) %all-gather.20.cloned.1.call-update) | async-done | bytes 16777232 | tf_op jit(solution)/shard_map/all_gather | solution.py:129
  335.5 7.8 %fusion.4 = f32[256,4096]{1,0:T(8,128)} fusion(bf16[2,1024,4096]{2,1,0:T(8,128)(2,1)} %all-gather.20.cloned.1.call-done, bf16[32,8,8,128]{3,2,1,0:T(8,128)(2,1)S(1)} %bitcast.123), kind=kOutput, calls=%fused_computation.10 | convolution fusion | flops 2147483648 | bytes 13107200 | tf_op jit(solution)/shard_map/dot_general | solution.py:50
  343.3 57.7 %reduce-scatter.6.cloned.1.call-done = f32[256,2048]{1,0:T(8,128)} async-done(((f32[256,4096]{1,0:T(8,128)}), f32[256,2048]{1,0:T(8,128)}) %reduce-scatter.6.cloned.1.call-update) | async-done | bytes 2097168 | tf_op jit(solution)/shard_map/reduce_scatter | solution.py:51
  401.1 2.8 add_convert_fusion.1
  404.0 0.3 reduce-scatter.8.cloned.1.call-start
  404.2 4.5 convert_bitcast_fusion
  408.8 0.6 copy.124
  409.4 0.9 copy-done.12
  410.3 2.3 convert_bitcast_fusion.1
  412.6 2.0 copy.125
  414.6 26.1 %all-gather.22.cloned.1.call-done = bf16[256,4096]{1,0:T(8,128)(2,1)} async-done(((bf16[256,2048]{1,0:T(8,128)(2,1)}), bf16[256,4096]{1,0:T(8,128)(2,1)}) %all-gather.22.cloned.1.call-update) | async-done | bytes 2097168 | tf_op jit(solution)/shard_map/all_gather | solution.py:29
  440.7 2.2 fusion.9
  442.9 5.8 %fusion.55 = bf16[32,8,8,128]{3,1,2,0:T(8,128)(2,1)S(1)} fusion(bf16[2,4096,1024]{2,1,0:T(8,128)(2,1)} %all-gather.16.cloned.1.call-done, bf16[256,4096]{1,0:T(8,128)(2,1)S(1)} %copy-done.8, f32[4096]{0:T(1024)S(1)} %bitcast.126, f32[256]{0:T(256)S(1)} %add_rsqrt_fusion), kind=kOutput, calls=%fused_computation.63 | convolution fusion | flops 2152202240 | bytes 11027456 | tf_op jit(solution)/shard_map/dot_general | solution.py:32
  448.9 0.8 fusion.16
  449.7 1.3 copy-done.4
  451.1 0.6 fusion.105
  451.7 1.0 copy-done.9
  452.6 5.9 %fusion.46 = bf16[4,64,8,128]{3,1,2,0:T(8,128)(2,1)S(1)} fusion(bf16[4,256,8,128]{3,2,1,0:T(8,128)(2,1)S(1)} %bitcast.116, f32[4,8,64]{2,1,0:T(8,128)S(1)} %fusion.105, f32[4,8,64,256]{3,2,1,0:T(8,128)} %copy-done.4), kind=kOutput, calls=%fused_computation.60 | convolution fusion | flops 136055040 | bytes 4726784 | tf_op jit(solution)/shard_map/chqk,ckhd->cqhd/dot_general | solution.py:46
  458.5 0.3 copy.100
  458.9 7.6 %fusion.2 = f32[256,4096]{1,0:T(8,128)} fusion(bf16[2,1024,4096]{2,1,0:T(8,128)(2,1)} %all-gather.20.cloned.1.call-done, bf16[32,8,8,128]{3,2,1,0:T(8,128)(2,1)S(1)} %bitcast.124), kind=kOutput, calls=%fused_computation.6 | convolution fusion | flops 2147483648 | bytes 13107200 | tf_op jit(solution)/shard_map/dot_general | solution.py:50
  466.6 58.0 %reduce-scatter.8.cloned.1.call-done = f32[256,2048]{1,0:T(8,128)} async-done(((f32[256,4096]{1,0:T(8,128)}), f32[256,2048]{1,0:T(8,128)}) %reduce-scatter.8.cloned.1.call-update) | async-done | bytes 2097168 | tf_op jit(solution)/shard_map/reduce_scatter | solution.py:51
  524.6 2.8 add_convert_fusion
  (81 shorter events, 2.4 us)
Async XLA Ops:
  6.5 3.1 copy-start
  6.5 3.1 copy-start.16
  6.5 35.9 %all-reduce.2.cloned.1.call-start = ((), (), s32[]{:S(2)}) async-start(), calls=%async_computation.4 | async-start | bytes 3670016 | tf_op jit(solution)/shard_map/psum | solution.py:81
  12.2 32.4 %copy-start.14 = (s32[256,2]{0,1:T(2,128)S(1)}, s32[256,2]{0,1:T(2,128)}, u32[]{:S(2)}) copy-start(s32[256,2]{0,1:T(2,128)} %param.13) | copy-start | bytes 6148
  12.2 54.8 %reduce-scatter.4.cloned.1.call-start = ((), (), s32[]{:S(2)}) async-start(), calls=%async_computation.5 | async-start | bytes 1376256 | tf_op jit(solution)/shard_map/reduce_scatter | solution.py:84
  44.6 25.6 %copy-start.5 = (bf16[4,128,896]{2,1,0:T(8,128)(2,1)S(1)}, bf16[4,128,896]{2,1,0:T(8,128)(2,1)}, u32[]{:S(2)}) copy-start(bf16[4,128,896]{2,1,0:T(8,128)(2,1)} %param.12) | copy-start | bytes 2752516
  73.1 57.9 %all-to-all-start = ((bf16[32,64,896]{2,1,0:T(8,128)(2,1)}), bf16[32,64,896]{2,1,0:T(8,128)(2,1)}, u32[]{:S(2)}, u32[]{:S(2)}) async-start(bf16[32,64,896]{2,1,0:T(8,128)(2,1)} %gather_fusion), calls=%async_computation.1 | async-start | bytes 7340032 | tf_op jit(solution)/shard_map/all_to_all | solution.py:106
  82.3 52.4 %copy-start.6 = (bf16[512,2048]{1,0:T(8,128)(2,1)S(1)}, bf16[512,2048]{1,0:T(8,128)(2,1)}, u32[]{:S(2)}) copy-start(bf16[512,2048]{1,0:T(8,128)(2,1)} %param.11) | copy-start | bytes 6291460
  82.3 87.7 %all-gather.24.cloned.1.call-start = ((), (), s32[]{:S(2)}) async-start(), calls=%async_computation.14 | async-start | bytes 2752512 | tf_op jit(solution)/shard_map/all_gather | solution.py:116
  134.6 73.5 %all-gather.14.cloned.1.call-start = ((), (), s32[]{:S(2)}) async-start(), calls=%async_computation.7 | async-start | bytes 3145728 | tf_op jit(solution)/shard_map/all_gather | solution.py:29
  135.7 91.1 %all-gather.26.cloned.1.call-start = ((), (), s32[]{:S(2)}) async-start(), calls=%async_computation.15 | async-start | bytes 5505024 | tf_op jit(solution)/shard_map/all_gather | solution.py:117
  170.0 75.3 %all-gather.18.cloned.1.call-start = ((), (), s32[]{:S(2)}) async-start(), calls=%async_computation.9 | async-start | bytes 5505024 | tf_op jit(solution)/shard_map/all_gather | solution.py:127
  170.6 93.3 %all-gather.12.cloned.1.call-start = ((), (), s32[]{:S(2)}) async-start(), calls=%async_computation.6 | async-start | bytes 5505024 | tf_op jit(solution)/shard_map/all_gather | solution.py:128
  171.3 128.4 %all-gather.16.cloned.1.call-start = ((), (), s32[]{:S(2)}) async-start(), calls=%async_computation.8 | async-start | bytes 25165824 | tf_op jit(solution)/shard_map/all_gather | solution.py:126
  172.1 0.8 copy-start.13
  172.1 163.4 %all-gather.20.cloned.1.call-start = ((), (), s32[]{:S(2)}) async-start(), calls=%async_computation.10 | async-start | bytes 25165824 | tf_op jit(solution)/shard_map/all_gather | solution.py:129
  172.8 228.2 %reduce-scatter.6.cloned.1.call-start = ((), (), s32[]{:S(2)}) async-start(), calls=%async_computation.11 | async-start | bytes 6291456 | tf_op jit(solution)/shard_map/reduce_scatter | solution.py:51
  229.7 15.6 %copy-start.11 = (bf16[8,128,896]{2,1,0:T(8,128)(2,1)}, bf16[8,128,896]{2,1,0:T(8,128)(2,1)S(1)}, u32[]{:S(2)}) copy-start(bf16[8,128,896]{2,1,0:T(8,128)(2,1)S(1)} %gather_fusion.2) | copy-start | bytes 5505028
  307.1 1.4 copy-start.3
  308.4 1.6 copy-start.10
  343.3 57.8 %copy-start.7 = (bf16[512,2048]{1,0:T(8,128)(2,1)S(1)}, bf16[512,2048]{1,0:T(8,128)(2,1)}, u32[]{:S(2)}) copy-start(bf16[512,2048]{1,0:T(8,128)(2,1)} %param.11) | copy-start | bytes 6291460
  343.3 97.4 %all-gather.22.cloned.1.call-start = ((), (), s32[]{:S(2)}) async-start(), calls=%async_computation.12 | async-start | bytes 3145728 | tf_op jit(solution)/shard_map/all_gather | solution.py:29
  404.0 120.6 %reduce-scatter.8.cloned.1.call-start = ((), (), s32[]{:S(2)}) async-start(), calls=%async_computation.13 | async-start | bytes 6291456 | tf_op jit(solution)/shard_map/reduce_scatter | solution.py:51
  404.2 5.2 copy-start.15
  408.8 1.5 copy-start.12
  440.7 2.2 copy-start.8
  449.7 1.4 copy-start.4
  451.1 1.6 copy-start.9
  466.5 58.0 %copy-start.2 = (bf16[256,2048]{1,0:T(8,128)(2,1)S(1)}, bf16[256,2048]{1,0:T(8,128)(2,1)}, u32[]{:S(2)}) copy-start(bf16[256,2048]{1,0:T(8,128)(2,1)} %add_convert_fusion.1) | copy-start | bytes 3145732
  466.6 60.9 %copy-start.1 = (bf16[512,896]{1,0:T(8,128)(2,1)S(1)}, bf16[512,896]{1,0:T(8,128)(2,1)}, u32[]{:S(2)}) copy-start(bf16[512,896]{1,0:T(8,128)(2,1)} %param.16) | copy-start | bytes 2752516
Sparse Core Ops, SparseCore 0:
  12.4 30.0 all-reduce.1
  44.8 22.2 reduce-scatter.3
  134.7 35.2 all-gather.23
  171.5 36.5 all-gather.13
  209.6 17.1 all-gather.25
  228.3 16.9 all-gather.17
  246.9 16.9 all-gather.11
  265.6 34.1 all-gather.15
  301.4 34.1 all-gather.19
  343.4 57.6 reduce-scatter.5
  404.1 36.5 all-gather.21
  466.7 57.8 reduce-scatter.7

commit v2 on v1

--- a/solution.py
+++ b/solution.py
@@ -24,9 +24,31 @@
     return jnp.dot(inner_act, enc_down, preferred_element_type=jnp.float32)
 
 
+def swap(block, axis):
+    return lax.ppermute(block, axis, [(0, 1), (1, 0)])
+
+
+def pair_gather(block, axis, dim):
+    other = swap(block, axis)
+    first = lax.axis_index(axis) == 0
+    return jnp.where(
+        first,
+        jnp.concatenate([block, other], axis=dim),
+        jnp.concatenate([other, block], axis=dim),
+    )
+
+
+def pair_scatter_sum(block, axis, dim, link_type):
+    index = lax.axis_index(axis)
+    half = block.shape[dim] // 2
+    mine = lax.dynamic_slice_in_dim(block, index * half, half, dim)
+    theirs = lax.dynamic_slice_in_dim(block, (1 - index) * half, half, dim)
+    return mine + swap(theirs.astype(link_type), axis).astype(mine.dtype)
+
+
 def cross_layer(state_rows, blocks, gain_vec, query_w, key_w, value_w, out_w):
     block_count = blocks.shape[0]
-    whole_rows = lax.all_gather(state_rows, "mp", axis=1, tiled=True)
+    whole_rows = pair_gather(state_rows, "mp", 1)
     floats = whole_rows.astype(jnp.float32)
     normed = rms_scale(floats, gain_vec).astype(jnp.bfloat16)
     queries = (jnp.dot(normed, query_w, preferred_element_type=jnp.float32) * HD ** (-0.5)).astype(
@@ -48,7 +70,7 @@
     )
     context = context.astype(jnp.bfloat16).reshape(block_count * QBLOCK, head_count * HD)
     partial_out = jnp.dot(context, out_w, preferred_element_type=jnp.float32)
-    head_share = lax.psum_scatter(partial_out, "mp", scatter_dimension=1, tiled=True)
+    head_share = pair_scatter_sum(partial_out, "mp", 1, jnp.bfloat16)
     return (state_rows.astype(jnp.float32) + head_share).astype(jnp.bfloat16)
 
 
@@ -78,11 +100,12 @@
     quarter = half_rows // channels
 
     held_rows = database.reshape(-1, E).astype(jnp.float32)
-    terms = lax.psum(encoder_terms(held_rows, enc_gain, enc_up, enc_down), "section")
+    terms = encoder_terms(held_rows, enc_gain, enc_up, enc_down)
+    terms = terms + swap(terms, "section")
     terms = terms.reshape(blocks_held, halves, channels, quarter, E)
     terms = lax.dynamic_index_in_dim(terms, sec_index, 2, keepdims=False)
-    terms = lax.psum_scatter(terms, "mp", scatter_dimension=1, tiled=True)
-    terms = lax.all_gather(terms, "section", axis=2, tiled=True)
+    terms = pair_scatter_sum(terms, "mp", 1, jnp.float32)
+    terms = pair_gather(terms, "section", 2)
     terms = terms.reshape(blocks_held, half_rows, E)
     own_rows = lax.dynamic_slice_in_dim(database, mp_index * half_rows, half_rows, 1)
     enc_half = (own_rows.astype(jnp.float32) + terms).astype(jnp.bfloat16)
@@ -113,8 +136,8 @@
     )
     slot_owner = jnp.sum(jnp.where(pick, my_owner[None, :], 0), axis=-1)
     compact = received[slot_owner]
-    channel_blocks = lax.all_gather(compact, "mp", axis=1, tiled=True)
-    all_blocks = lax.all_gather(channel_blocks, "section", axis=0, tiled=True)
+    channel_blocks = pair_gather(compact, "mp", 1)
+    all_blocks = pair_gather(channel_blocks, "section", 0)
     flat_pos = my_channel * per_channel + my_slot
     mine = lax.dynamic_slice_in_dim(flat_pos, sec_index * per_channel, per_channel, 0)
     neighbours = all_blocks[mine]

time: 535 us -> 308 us (0.58)
  waiting for transfers between devices: 404 us -> 161 us
  starting transfers between devices: 9.86 us -> 23.1 us
  matrix products: 59.7 us -> 53.7 us
    reduce_scatter x3 -> x0, waiting for transfers between devices: 136 us -> none  [the longest x2 116 us: cross_layer(): lax.psum_scatter(partial_out, 'mp', scatter_dimension=1, tiled=True)]
    ppermute x0 -> x9, waiting for transfers between devices: none -> 111 us  [swap(): return lax.ppermute(block, axis, [(0, 1), (1, 0)])]
    all_gather x4 -> x0, waiting for transfers between devices: 110 us -> none  [the longest x2 58.7 us: cross_layer(): whole_rows = lax.all_gather(state_rows, 'mp', axis=1, tiled=True)]
    psum x1 -> x0, waiting for transfers between devices: 30.1 us -> none  [body(): lax.psum(encoder_terms(held_rows, enc_gain, enc_up, enc_down), 'section')]
    all_gather x1, waiting for transfers between devices: 29.5 us -> 0.01 us  [body(): wq = lax.all_gather(w_query, 'section', axis=0, tiled=True)]
    all_gather x1, waiting for transfers between devices: 18.3 us -> 0.02 us  [body(): wo = lax.all_gather(w_out, 'section', axis=0, tiled=True)]
    all_gather x1, waiting for transfers between devices: 15.6 us -> 0.02 us  [body(): wk = lax.all_gather(w_key, 'section', axis=0, tiled=True)]
    all_gather x1, waiting for transfers between devices: 14.2 us -> 0.02 us  [body(): wv = lax.all_gather(w_value, 'section', axis=0, tiled=True)]
  transfers between devices with their start and end apart: 13 -> 14, of which waited for: 13 -> 9; matrix products, arithmetic and copies ran while one was open for 8% -> 22% of each run, Pallas kernels for 0% -> 0%
where the time goes in v2:
time: 308 us; the launch traced here: 303 us
  waiting for transfers between devices  161 us (52%)
  matrix products  53.7 us (17%)
  local copies, waits for them, and re-layouts  29.2 us (9%)
  starting transfers between devices  23.1 us (8%)
  other arithmetic  20.1 us (7%)
  between operations  13.7 us (4%)
    ppermute x9, waiting for transfers between devices, swap(): return lax.ppermute(block, axis, [(0, 1), (1, 0)])  111 us
    all_to_all x1, waiting for transfers between devices, body(): lax.all_to_all(payload, 'db', split_axis=0, concat_axis=0, tiled=True)  47.9 us
    unnamed x43, local copies, waits for them, and re-layouts  15.7 us
    dot_general x2, matrix products, cross_layer(): jnp.einsum('chqk,ckhd->cqhd', soft_weights, value_four, preferred_element...  12.4 us
    ppermute x9, starting transfers between devices, swap(): return lax.ppermute(block, axis, [(0, 1), (1, 0)])  12 us
    dot_general x2, matrix products, cross_layer(): partial_out = jnp.dot(context, out_w, preferred_element_type=jnp.float32)  11.7 us
    all_to_all x1, starting transfers between devices, body(): lax.all_to_all(payload, 'db', split_axis=0, concat_axis=0, tiled=True)  11 us
    dot_general x2, matrix products, cross_layer(): jnp.dot(normed, query_w, preferred_element_type=jnp.float32) * HD ** (-0.5)  9.57 us
  transfers between devices with their start and end apart: 14, of which 9 were waited for; matrix products, arithmetic and copies ran while one was open for 22% of the time, Pallas kernels for 0%

profile of v2, /device:TPU:1, one launch (start us, length us, event | category | flops | bytes accessed | tf_op | source)
XLA Modules:
  0.0 302.9 jit_solution(12955998072685671519)
XLA Ops:
  6.5 0.7 all-gather.10.cloned.1.call-update
  7.3 0.7 all-gather.6.cloned.1.call-update
  8.1 0.7 all-gather.8.cloned.1.call-update
  8.8 0.5 all-gather.12.cloned.1.call-update
  9.3 0.6 copy-done.4
  10.5 3.9 %fusion.70 = f32[512,896]{1,0:T(8,128)} fusion(bf16[512,896]{1,0:T(8,128)(2,1)S(1)} %copy-done, bf16[512,896]{1,0:T(8,128)(2,1)S(1)} %fusion.27, bf16[896,512]{1,0:T(8,128)(2,1)} %param.15), kind=kOutput, calls=%fused_computation.83 | convolution fusion | flops 941883392 | bytes 4587520 | tf_op jit(solution)/shard_map/dot_general | solution.py:24
  14.4 1.4 collective-permute-start
  16.1 3.4 %collective-permute-done = f32[512,896]{1,0:T(8,128)} collective-permute-done((f32[512,896]{1,0:T(8,128)}, f32[512,896]{1,0:T(8,128)}, u32[]{:S(2)}, u32[]{:S(2)}) %collective-permute-start) | collective-permute-done | bytes 1835040 | tf_op jit(solution)/shard_map/ppermute | solution.py:28
  19.5 2.5 add.170
  22.0 1.3 copy-done.5
  23.3 1.4 collective-permute-start.1
  25.7 9.4 %collective-permute-done.1 = f32[4,1,32,896]{3,2,0,1:T(8,128)S(1)} collective-permute-done((f32[4,1,32,896]{3,2,0,1:T(8,128)S(1)}, f32[4,1,32,896]{3,2,0,1:T(8,128)S(1)}, u32[]{:S(2)}, u32[]{:S(2)}) %collective-permute-start.1) | collective-permute-done | bytes 458784 | tf_op jit(solution)/shard_map/ppermute | solution.py:28
  35.1 1.1 bitcast_add_fusion
  36.2 1.3 collective-permute-start.2
  38.0 0.9 collective-permute-done.2
  39.0 2.9 gather_fusion
  41.9 11.0 %all-to-all-start = ((bf16[32,64,896]{2,1,0:T(8,128)(2,1)}), bf16[32,64,896]{2,1,0:T(8,128)(2,1)}, u32[]{:S(2)}, u32[]{:S(2)}) async-start(bf16[32,64,896]{2,1,0:T(8,128)(2,1)} %gather_fusion), calls=%async_computation | async-start | bytes 7340032 | tf_op jit(solution)/shard_map/all_to_all | solution.py:129
  53.7 47.9 %all-to-all-done = bf16[32,64,896]{2,1,0:T(8,128)(2,1)} async-done(((bf16[32,64,896]{2,1,0:T(8,128)(2,1)}), bf16[32,64,896]{2,1,0:T(8,128)(2,1)}, u32[]{:S(2)}, u32[]{:S(2)}) %all-to-all-start) | async-done | bytes 3670048 | tf_op jit(solution)/shard_map/all_to_all | solution.py:129
  101.6 3.3 %gather_fusion.1 = bf16[8,64,896]{2,1,0:T(8,128)(2,1)S(1)} fusion(bf16[32,64,896]{2,1,0:T(8,128)(2,1)} %all-to-all-done, s32[1024]{0:T(1024)S(1)} %pad_clamp_fusion.1), kind=kCustom, calls=%fused_computation.1 | custom fusion | bytes 1835040 | tf_op jit(solution)/shard_map/gather | solution.py:138
  104.9 1.2 collective-permute-start.3
  106.1 19.7 %collective-permute-done.3 = bf16[8,64,896]{2,1,0:T(8,128)(2,1)} collective-permute-done((bf16[8,64,896]{2,1,0:T(8,128)(2,1)S(1)}, bf16[8,64,896]{2,1,0:T(8,128)(2,1)}, u32[]{:S(2)}, u32[]{:S(2)}) %collective-permute-start.3) | collective-permute-done | bytes 917536 | tf_op jit(solution)/shard_map/ppermute | solution.py:28
  125.8 2.1 maximum_select_fusion.3
  127.8 2.2 collective-permute-start.4
  130.0 2.3 constant_dynamic-slice_fusion
  132.3 1.1 collective-permute-start.5
  133.5 1.8 all-gather
  135.4 22.0 %collective-permute-done.5 = bf16[256,2048]{1,0:T(8,128)(2,1)} collective-permute-done((bf16[256,2048]{1,0:T(8,128)(2,1)}, bf16[256,2048]{1,0:T(8,128)(2,1)}, u32[]{:S(2)}, u32[]{:S(2)}) %collective-permute-start.5) | collective-permute-done | bytes 1048608 | tf_op jit(solution)/shard_map/ppermute | solution.py:28
  157.4 3.0 fusion.6
  160.4 3.7 %maximum_select_fusion = bf16[16,128,896]{2,1,0:T(8,128)(2,1)} fusion(bf16[8,128,896]{2,1,0:T(8,128)(2,1)} %collective-permute-done.4, bf16[8,128,896]{2,1,0:T(8,128)(2,1)S(1)} %maximum_select_fusion.3, pred[]{:T(512)S(6)} %eq.92), kind=kLoop, calls=%fused_computation.23 | loop fusion | flops 5505024 | bytes 7340033 | tf_op jit(solution)/shard_map/jit(_where)/select_n | solution.py:34
  164.1 2.9 gather_fusion.2
  167.0 1.3 copy-done.8
  168.3 3.8 %convert_bitcast_fusion.2 = bf16[128,8,8,128]{3,1,2,0:T(8,128)(2,1)S(1)} fusion(bf16[1024,896]{1,0:T(8,128)(2,1)S(1)} %bitcast.120, bf16[2,896,1024]{2,1,0:T(8,128)(2,1)} %all-gather.10.cloned.1.call-done), kind=kOutput, calls=%fused_computation.46 | convolution fusion | flops 1880096768 | bytes 5767168 | tf_op jit(solution)/shard_map/dot_general | solution.py:58
  172.1 0.6 copy.129
  172.8 4.4 %convert_bitcast_fusion.3 = bf16[128,8,8,128]{3,1,2,0:T(8,128)(2,1)S(1)} fusion(bf16[1024,896]{1,0:T(8,128)(2,1)} %bitcast.121, bf16[2,896,1024]{2,1,0:T(8,128)(2,1)} %all-gather.6.cloned.1.call-done), kind=kOutput, calls=%fused_computation.49 | convolution fusion | flops 1880096768 | bytes 5767168 | tf_op jit(solution)/shard_map/dot_general | solution.py:59
  177.2 1.9 copy.130
  179.1 7.1 %fusion.52 = bf16[32,8,8,128]{3,1,2,0:T(8,128)(2,1)S(1)} fusion(bf16[2,4096,1024]{2,1,0:T(8,128)(2,1)} %all-gather.8.cloned.1.call-done, f32[4096]{0:T(1024)S(1)} %bitcast.130, f32[256]{0:T(256)S(1)} %add_rsqrt_fusion.1, bf16[256,2048]{1,0:T(8,128)(2,1)} %collective-permute-done.5, bf16[256,2048]{1,0:T(8,128)(2,1)} %constant_dynamic-slice_fusion, pred[]{:T(512)S(6)} %eq.93), kind=kOutput, calls=%fused_computation.68 | convolution fusion | flops 2161639424 | bytes 11027457 | tf_op jit(solution)/shard_map/dot_general | solution.py:54
  186.3 0.8 fusion.20
  187.1 1.3 copy-done.2
  188.5 0.6 fusion.107
  189.1 1.0 copy-done.7
  190.1 5.9 %fusion.49 = bf16[4,64,8,128]{3,1,2,0:T(8,128)(2,1)S(1)} fusion(bf16[4,256,8,128]{3,2,1,0:T(8,128)(2,1)S(1)} %bitcast.119, f32[4,8,64]{2,1,0:T(8,128)S(1)} %fusion.107, f32[4,8,64,256]{3,2,1,0:T(8,128)} %copy-done.2), kind=kOutput, calls=%fused_computation.67 | convolution fusion | flops 136055040 | bytes 4726784 | tf_op jit(solution)/shard_map/chqk,ckhd->cqhd/dot_general | solution.py:68
  196.0 0.3 copy.91
  196.4 5.9 %fusion.4 = f32[256,4096]{1,0:T(8,128)S(1)} fusion(bf16[2,1024,4096]{2,1,0:T(8,128)(2,1)} %all-gather.12.cloned.1.call-done, bf16[32,8,8,128]{3,2,1,0:T(8,128)(2,1)S(1)} %bitcast.125), kind=kOutput, calls=%fused_computation.10 | convolution fusion | flops 2147483648 | bytes 13107200 | tf_op jit(solution)/shard_map/dot_general | solution.py:72
  202.3 2.0 copy-done.6
  204.4 1.2 collective-permute-start.6
  205.6 22.7 %collective-permute-done.6 = bf16[256,2048]{1,0:T(8,128)(2,1)S(1)} collective-permute-done((bf16[256,2048]{1,0:T(8,128)(2,1)S(1)}, bf16[256,2048]{1,0:T(8,128)(2,1)S(1)}, u32[]{:S(2)}, u32[]{:S(2)}) %collective-permute-start.6) | collective-permute-done | bytes 1048608 | tf_op jit(solution)/shard_map/ppermute | solution.py:28
  228.4 2.3 add_convert_fusion.1
  230.7 1.2 collective-permute-start.7
  231.9 4.0 %convert_bitcast_fusion = bf16[128,8,8,128]{3,1,2,0:T(8,128)(2,1)S(1)} fusion(bf16[1024,896]{1,0:T(8,128)(2,1)S(1)} %bitcast.122, bf16[2,896,1024]{2,1,0:T(8,128)(2,1)} %all-gather.10.cloned.1.call-done), kind=kOutput, calls=%fused_computation.38 | convolution fusion | flops 1880096768 | bytes 5767168 | tf_op jit(solution)/shard_map/dot_general | solution.py:58
  235.9 0.6 copy.133
  236.5 1.4 copy-done.13
  237.9 2.3 convert_bitcast_fusion.1
  240.3 1.9 copy.134
  242.2 11.5 %collective-permute-done.7 = bf16[256,2048]{1,0:T(8,128)(2,1)S(1)} collective-permute-done((bf16[256,2048]{1,0:T(8,128)(2,1)S(1)}, bf16[256,2048]{1,0:T(8,128)(2,1)S(1)}, u32[]{:S(2)}, u32[]{:S(2)}) %collective-permute-start.7) | collective-permute-done | bytes 1048608 | tf_op jit(solution)/shard_map/ppermute | solution.py:28
  253.7 0.6 fusion.9
  254.4 2.5 fusion.55
  257.1 0.8 fusion.16
  257.9 1.3 copy-done.3
  259.3 0.6 fusion.108
  259.9 6.5 %fusion.46 = bf16[4,64,8,128]{3,1,2,0:T(8,128)(2,1)S(1)} fusion(bf16[4,256,8,128]{3,2,1,0:T(8,128)(2,1)} %bitcast.118, f32[4,8,64]{2,1,0:T(8,128)S(1)} %fusion.108, f32[4,8,64,256]{3,2,1,0:T(8,128)} %copy-done.3), kind=kOutput, calls=%fused_computation.66 | convolution fusion | flops 136055040 | bytes 4726784 | tf_op jit(solution)/shard_map/chqk,ckhd->cqhd/dot_general | solution.py:68
  266.8 5.7 %fusion.2 = f32[256,4096]{1,0:T(8,128)S(1)} fusion(bf16[2,1024,4096]{2,1,0:T(8,128)(2,1)} %all-gather.12.cloned.1.call-done, bf16[32,8,8,128]{3,2,1,0:T(8,128)(2,1)S(1)} %bitcast.126), kind=kOutput, calls=%fused_computation.6 | convolution fusion | flops 2147483648 | bytes 13107200 | tf_op jit(solution)/shard_map/dot_general | solution.py:72
  272.7 1.2 collective-permute-start.8
  273.8 21.0 %collective-permute-done.8 = bf16[256,2048]{1,0:T(8,128)(2,1)S(1)} collective-permute-done((bf16[256,2048]{1,0:T(8,128)(2,1)S(1)}, bf16[256,2048]{1,0:T(8,128)(2,1)S(1)}, u32[]{:S(2)}, u32[]{:S(2)}) %collective-permute-start.8) | collective-permute-done | bytes 1048608 | tf_op jit(solution)/shard_map/ppermute | solution.py:28
  294.9 1.5 add_convert_fusion
  (83 shorter events, 4.4 us)
Async XLA Ops:
  6.5 3.9 %copy-start = (bf16[512,896]{1,0:T(8,128)(2,1)S(1)}, bf16[512,896]{1,0:T(8,128)(2,1)}, u32[]{:S(2)}) copy-start(bf16[512,896]{1,0:T(8,128)(2,1)} %param.16) | copy-start | bytes 2752516
  6.5 160.5 %all-gather.10.cloned.1.call-start = ((), (), s32[]{:S(2)}) async-start(), calls=%async_computation.3 | async-start | bytes 5505024 | tf_op jit(solution)/shard_map/all_gather | solution.py:150
  7.3 165.5 %all-gather.6.cloned.1.call-start = ((), (), s32[]{:S(2)}) async-start(), calls=%async_computation.1 | async-start | bytes 5505024 | tf_op jit(solution)/shard_map/all_gather | solution.py:151
  8.0 171.1 %all-gather.8.cloned.1.call-start = ((), (), s32[]{:S(2)}) async-start(), calls=%async_computation.2 | async-start | bytes 25165824 | tf_op jit(solution)/shard_map/all_gather | solution.py:149
  8.7 1.2 copy-start.4
  8.8 1.4 copy-start.12
  8.8 187.6 %all-gather.12.cloned.1.call-start = ((), (), s32[]{:S(2)}) async-start(), calls=%async_computation.4 | async-start | bytes 25165824 | tf_op jit(solution)/shard_map/all_gather | solution.py:152
  10.5 5.3 %copy-start.11 = (s32[256,2]{0,1:T(2,128)S(1)}, s32[256,2]{0,1:T(2,128)}, u32[]{:S(2)}) copy-start(s32[256,2]{0,1:T(2,128)} %param.13) | copy-start | bytes 6148
  14.4 5.1 %collective-permute-start = (f32[512,896]{1,0:T(8,128)}, f32[512,896]{1,0:T(8,128)}, u32[]{:S(2)}, u32[]{:S(2)}) collective-permute-start(f32[512,896]{1,0:T(8,128)} %fusion.70), channel_id=1, source_target_pairs={{0,2},{2,0},{1,3},{3,1},{4,6},{6,4},{5,7},{7,5},{8,10},{10,8},{9,1... | collective-permute-start | bytes 5505032 | tf_op jit(solution)/shard_map/ppermute | solution.py:28
  22.0 1.3 copy-start.5
  23.3 11.8 %collective-permute-start.1 = (f32[4,1,32,896]{3,2,0,1:T(8,128)S(1)}, f32[4,1,32,896]{3,2,0,1:T(8,128)S(1)}, u32[]{:S(2)}, u32[]{:S(2)}) collective-permute-start(f32[4,1,32,896]{3,2,0,1:T(8,128)S(1)} %dynamic-slice_bitcast_fusion), channel_id=1, source_target_pairs={{0,1},{1,0},{2,3},{3,2},{4,5},{5,4},{6,7},{7,6},{8,9},{9,8},{10,11... | collective-permute-start | bytes 1376264 | tf_op jit(solution)/shard_map/ppermute | solution.py:28
  36.2 2.7 collective-permute-start.2
  41.9 59.7 %all-to-all-start = ((bf16[32,64,896]{2,1,0:T(8,128)(2,1)}), bf16[32,64,896]{2,1,0:T(8,128)(2,1)}, u32[]{:S(2)}, u32[]{:S(2)}) async-start(bf16[32,64,896]{2,1,0:T(8,128)(2,1)} %gather_fusion), calls=%async_computation | async-start | bytes 7340032 | tf_op jit(solution)/shard_map/all_to_all | solution.py:129
  104.9 20.8 %collective-permute-start.3 = (bf16[8,64,896]{2,1,0:T(8,128)(2,1)S(1)}, bf16[8,64,896]{2,1,0:T(8,128)(2,1)}, u32[]{:S(2)}, u32[]{:S(2)}) collective-permute-start(bf16[8,64,896]{2,1,0:T(8,128)(2,1)S(1)} %gather_fusion.1), channel_id=1, source_target_pairs={{0,1},{1,0},{2,3},{3,2},{4,5},{5,4},{6,7},{7,6},{8,9},{9,8},{10,11... | collective-permute-start | bytes 2752520 | tf_op jit(solution)/shard_map/ppermute | solution.py:28
  106.1 27.4 %copy-start.10 = (f32[1,4096]{1,0:T(1,128)S(1)}, f32[1,4096]{1,0:T(1,128)}, u32[]{:S(2)}) copy-start(f32[1,4096]{1,0:T(1,128)} %param.17) | copy-start | bytes 49156
  127.8 32.5 %collective-permute-start.4 = (bf16[8,128,896]{2,1,0:T(8,128)(2,1)S(1)}, bf16[8,128,896]{2,1,0:T(8,128)(2,1)}, u32[]{:S(2)}, u32[]{:S(2)}) collective-permute-start(bf16[8,128,896]{2,1,0:T(8,128)(2,1)S(1)} %maximum_select_fusion.3), channel_id=1, source_target_pairs={{0,2},{2,0},{1,3},{3,1},{4,6},{6,4},{5,7},{7,5},{8,10},{10,8},{9,1... | collective-permute-start | bytes 5505032 | tf_op jit(solution)/shard_map/ppermute | solution.py:28
  132.3 25.0 %collective-permute-start.5 = (bf16[256,2048]{1,0:T(8,128)(2,1)}, bf16[256,2048]{1,0:T(8,128)(2,1)}, u32[]{:S(2)}, u32[]{:S(2)}) collective-permute-start(bf16[256,2048]{1,0:T(8,128)(2,1)} %constant_dynamic-slice_fusion), channel_id=1, source_target_pairs={{0,1},{1,0},{2,3},{3,2},{4,5},{5,4},{6,7},{7,6},{8,9},{9,8},{10,11... | collective-permute-start | bytes 3145736 | tf_op jit(solution)/shard_map/ppermute | solution.py:28
  167.0 1.3 copy-start.8
  187.1 1.4 copy-start.2
  188.5 1.6 copy-start.7
  202.3 2.0 copy-start.6
  204.4 23.9 %collective-permute-start.6 = (bf16[256,2048]{1,0:T(8,128)(2,1)S(1)}, bf16[256,2048]{1,0:T(8,128)(2,1)S(1)}, u32[]{:S(2)}, u32[]{:S(2)}) collective-permute-start(bf16[256,2048]{1,0:T(8,128)(2,1)S(1)} %dynamic-slice_convert_fusion.1), channel_id=1, source_target_pairs={{0,1},{1,0},{2,3},{3,2},{4,5},{5,4},{6,7},{7,6},{8,9},{9,8},{10,11... | collective-permute-start | bytes 3145736 | tf_op jit(solution)/shard_map/ppermute | solution.py:28
  205.6 26.3 %copy-start.9 = (bf16[8,128,896]{2,1,0:T(8,128)(2,1)S(1)}, bf16[8,128,896]{2,1,0:T(8,128)(2,1)}, u32[]{:S(2)}) copy-start(bf16[8,128,896]{2,1,0:T(8,128)(2,1)} %copy-done.8) | copy-start | bytes 5505028
  230.7 23.1 %collective-permute-start.7 = (bf16[256,2048]{1,0:T(8,128)(2,1)S(1)}, bf16[256,2048]{1,0:T(8,128)(2,1)S(1)}, u32[]{:S(2)}, u32[]{:S(2)}) collective-permute-start(bf16[256,2048]{1,0:T(8,128)(2,1)S(1)} %add_convert_fusion.1), channel_id=1, source_target_pairs={{0,1},{1,0},{2,3},{3,2},{4,5},{5,4},{6,7},{7,6},{8,9},{9,8},{10,11... | collective-permute-start | bytes 3145736 | tf_op jit(solution)/shard_map/ppermute | solution.py:28
  231.9 22.5 %slice-start = ((s8[16777216]{0:T(1024)(128)(4,1)}), s8[4194304]{0:T(1024)(128)(4,1)S(1)}, s32[]{:S(2)}) async-start(s8[16777216]{0:T(1024)(128)(4,1)} %bitcast.131), calls=%async_computation.5 | async-start | bytes 8388608
  231.9 22.5 %slice-start.1 = ((s8[16777216]{0:T(1024)(128)(4,1)}), s8[4194304]{0:T(1024)(128)(4,1)S(1)}, s32[]{:S(2)}) async-start(s8[16777216]{0:T(1024)(128)(4,1)} %bitcast.131), calls=%async_computation.6 | async-start | bytes 8388608
  235.9 2.0 copy-start.13
  237.9 16.5 %slice-start.2 = ((s8[16777216]{0:T(1024)(128)(4,1)}), s8[4194304]{0:T(1024)(128)(4,1)S(1)}, s32[]{:S(2)}) async-start(s8[16777216]{0:T(1024)(128)(4,1)} %bitcast.131), calls=%async_computation.7 | async-start | bytes 8388608
  237.9 16.5 %slice-start.3 = ((s8[16777216]{0:T(1024)(128)(4,1)}), s8[4194304]{0:T(1024)(128)(4,1)S(1)}, s32[]{:S(2)}) async-start(s8[16777216]{0:T(1024)(128)(4,1)} %bitcast.131), calls=%async_computation.8 | async-start | bytes 8388608
  257.9 1.4 copy-start.3
  272.5 23.9 %copy-start.1 = (bf16[512,896]{1,0:T(8,128)(2,1)S(1)}, bf16[512,896]{1,0:T(8,128)(2,1)}, u32[]{:S(2)}) copy-start(bf16[512,896]{1,0:T(8,128)(2,1)} %param.16) | copy-start | bytes 2752516
  272.7 22.2 %collective-permute-start.8 = (bf16[256,2048]{1,0:T(8,128)(2,1)S(1)}, bf16[256,2048]{1,0:T(8,128)(2,1)S(1)}, u32[]{:S(2)}, u32[]{:S(2)}) collective-permute-start(bf16[256,2048]{1,0:T(8,128)(2,1)S(1)} %dynamic-slice_convert_fusion), channel_id=1, source_target_pairs={{0,1},{1,0},{2,3},{3,2},{4,5},{5,4},{6,7},{7,6},{8,9},{9,8},{10,11... | collective-permute-start | bytes 3145736 | tf_op jit(solution)/shard_map/ppermute | solution.py:28
Sparse Core Ops, SparseCore 0:
  9.0 19.2 all-gather.9
  29.9 16.9 all-gather.5
  48.5 34.1 all-gather.7
  84.2 34.1 all-gather.11

commit v3 on v2

--- a/solution.py
+++ b/solution.py
@@ -46,14 +46,17 @@
     return mine + swap(theirs.astype(link_type), axis).astype(mine.dtype)
 
 
-def cross_layer(state_rows, blocks, gain_vec, query_w, key_w, value_w, out_w):
-    block_count = blocks.shape[0]
+def layer_queries(state_rows, gain_vec, query_w):
     whole_rows = pair_gather(state_rows, "mp", 1)
     floats = whole_rows.astype(jnp.float32)
     normed = rms_scale(floats, gain_vec).astype(jnp.bfloat16)
-    queries = (jnp.dot(normed, query_w, preferred_element_type=jnp.float32) * HD ** (-0.5)).astype(
+    return (jnp.dot(normed, query_w, preferred_element_type=jnp.float32) * HD ** (-0.5)).astype(
         jnp.bfloat16
     )
+
+
+def cross_layer(state_rows, queries, blocks, query_w, key_w, value_w, out_w):
+    block_count = blocks.shape[0]
     flat_rows = blocks.reshape(-1, E)
     key_rows = jnp.dot(flat_rows, key_w, preferred_element_type=jnp.float32).astype(jnp.bfloat16)
     value_rows = jnp.dot(flat_rows, value_w, preferred_element_type=jnp.float32).astype(
@@ -99,6 +102,15 @@
     half_rows = NBLOCK // halves
     quarter = half_rows // channels
 
+    wq = lax.all_gather(w_query, "section", axis=0, tiled=True)
+    gains = lax.all_gather(dec_gain, "section", axis=0, tiled=True)
+    wk = lax.all_gather(w_key, "section", axis=0, tiled=True)
+    wv = lax.all_gather(w_value, "section", axis=0, tiled=True)
+    wo = lax.all_gather(w_out, "section", axis=0, tiled=True)
+    micro_tokens = hidden_in.shape[0] // channels
+    state = lax.dynamic_slice_in_dim(hidden_in, sec_index * micro_tokens, micro_tokens, 0)
+    queries = layer_queries(state, gains[0], wq[0])
+
     held_rows = database.reshape(-1, E).astype(jnp.float32)
     terms = encoder_terms(held_rows, enc_gain, enc_up, enc_down)
     terms = terms + swap(terms, "section")
@@ -127,6 +139,7 @@
     send_local = jnp.sum(jnp.where(serve, within, 0), axis=-1)
     payload = enc_half[send_local]
     received = lax.all_to_all(payload, "db", split_axis=0, concat_axis=0, tiled=True)
+    received, queries = lax.optimization_barrier((received, queries))
 
     my_owner = lax.dynamic_index_in_dim(owners, db_index, 0, keepdims=False)
     my_channel = lax.dynamic_index_in_dim(channel, db_index, 0, keepdims=False)
@@ -143,16 +156,11 @@
     neighbours = all_blocks[mine]
     enc_blocks = neighbours.reshape(-1, NEIGH * NBLOCK, E)
 
-    micro_tokens = hidden_in.shape[0] // channels
-    state = lax.dynamic_slice_in_dim(hidden_in, sec_index * micro_tokens, micro_tokens, 0)
-    gains = lax.all_gather(dec_gain, "section", axis=0, tiled=True)
-    wq = lax.all_gather(w_query, "section", axis=0, tiled=True)
-    wk = lax.all_gather(w_key, "section", axis=0, tiled=True)
-    wv = lax.all_gather(w_value, "section", axis=0, tiled=True)
-    wo = lax.all_gather(w_out, "section", axis=0, tiled=True)
     for layer_id in range(wq.shape[0]):
+        if layer_id > 0:
+            queries = layer_queries(state, gains[layer_id], wq[layer_id])
         state = cross_layer(
-            state, enc_blocks, gains[layer_id], wq[layer_id], wk[layer_id], wv[layer_id], wo[layer_id]
+            state, queries, enc_blocks, wq[layer_id], wk[layer_id], wv[layer_id], wo[layer_id]
         )
     return state
 

time: 308 us -> 302 us (0.981)
    all_to_all x1, waiting for transfers between devices: 47.9 us -> 0.01 us  [body(): lax.all_to_all(payload, 'db', split_axis=0, concat_axis=0, tiled=True)]
    ppermute x9, waiting for transfers between devices: 111 us -> 158 us  [swap(): return lax.ppermute(block, axis, [(0, 1), (1, 0)])]
    unnamed x43 -> x49, local copies, waits for them, and re-layouts: 15.7 us -> 15.8 us
  transfers between devices with their start and end apart: 14 -> 14, of which waited for: 9 -> 9; matrix products, arithmetic and copies ran while one was open for 22% -> 20% of each run, Pallas kernels for 0% -> 0%
where the time goes in v3:
time: 302 us; the launch traced here: 299 us
  waiting for transfers between devices  161 us (53%)
  matrix products  52.2 us (17%)
  local copies, waits for them, and re-layouts  27.8 us (9%)
  starting transfers between devices  24.8 us (8%)
  other arithmetic  17.8 us (6%)
  between operations  13.7 us (5%)
    ppermute x9, waiting for transfers between devices, swap(): return lax.ppermute(block, axis, [(0, 1), (1, 0)])  158 us
    unnamed x49, local copies, waits for them, and re-layouts  15.8 us
    ppermute x9, starting transfers between devices, swap(): return lax.ppermute(block, axis, [(0, 1), (1, 0)])  13.4 us
    dot_general x2, matrix products, cross_layer(): jnp.einsum('chqk,ckhd->cqhd', soft_weights, value_four, preferred_element...  12.4 us
    dot_general x2, matrix products, cross_layer(): partial_out = jnp.dot(context, out_w, preferred_element_type=jnp.float32)  11.4 us
    all_to_all x1, starting transfers between devices, body(): lax.all_to_all(payload, 'db', split_axis=0, concat_axis=0, tiled=True)  11.2 us
    dot_general x2, matrix products, layer_queries(): jnp.dot(normed, query_w, preferred_element_type=jnp.float32) * HD ** (-0.5)  8.28 us
    dot_general x2, matrix products, cross_layer(): jnp.dot(flat_rows, key_w, preferred_element_type=jnp.float32)  7.82 us
  transfers between devices with their start and end apart: 14, of which 9 were waited for; matrix products, arithmetic and copies ran while one was open for 20% of the time, Pallas kernels for 0%

profile of v3, /device:TPU:1, one launch (start us, length us, event | category | flops | bytes accessed | tf_op | source)
XLA Modules:
  0.0 299.4 jit_solution(5921650662221758102)
XLA Ops:
  6.5 0.7 all-gather.6.cloned.1.call-update
  7.3 0.7 all-gather.10.cloned.1.call-update
  8.1 0.7 all-gather.8.cloned.1.call-update
  8.8 0.5 all-gather.12.cloned.1.call-update
  9.3 0.6 copy-done.4
  10.5 3.9 %fusion.67 = f32[512,896]{1,0:T(8,128)} fusion(bf16[512,896]{1,0:T(8,128)(2,1)S(1)} %copy-done, bf16[512,896]{1,0:T(8,128)(2,1)S(1)} %fusion.27, bf16[896,512]{1,0:T(8,128)(2,1)} %param.15), kind=kOutput, calls=%fused_computation.82 | convolution fusion | flops 941883392 | bytes 4587520 | tf_op jit(solution)/shard_map/dot_general | solution.py:24
  14.4 1.4 collective-permute-start
  16.1 3.4 %collective-permute-done = f32[512,896]{1,0:T(8,128)} collective-permute-done((f32[512,896]{1,0:T(8,128)}, f32[512,896]{1,0:T(8,128)}, u32[]{:S(2)}, u32[]{:S(2)}) %collective-permute-start) | collective-permute-done | bytes 1835040 | tf_op jit(solution)/shard_map/ppermute | solution.py:28
  19.5 2.7 add.170
  22.2 1.3 copy-done.5
  23.5 1.3 collective-permute-start.1
  25.9 9.5 %collective-permute-done.1 = f32[4,1,32,896]{3,2,0,1:T(8,128)S(1)} collective-permute-done((f32[4,1,32,896]{3,2,0,1:T(8,128)S(1)}, f32[4,1,32,896]{3,2,0,1:T(8,128)S(1)}, u32[]{:S(2)}, u32[]{:S(2)}) %collective-permute-start.1) | collective-permute-done | bytes 458784 | tf_op jit(solution)/shard_map/ppermute | solution.py:28
  35.4 1.2 bitcast_add_fusion
  36.6 1.1 collective-permute-start.2
  38.2 1.6 collective-permute-done.2
  39.9 2.9 gather_fusion
  42.8 11.2 %all-to-all-start = ((bf16[32,64,896]{2,1,0:T(8,128)(2,1)}), bf16[32,64,896]{2,1,0:T(8,128)(2,1)}, u32[]{:S(2)}, u32[]{:S(2)}) async-start(bf16[32,64,896]{2,1,0:T(8,128)(2,1)} %gather_fusion), calls=%async_computation | async-start | bytes 7340032 | tf_op jit(solution)/shard_map/all_to_all | solution.py:141
  54.1 1.3 constant_dynamic-slice_fusion
  56.3 0.7 multiply_reduce_fusion.1
  57.1 2.4 all-gather
  59.6 0.6 pad_clamp_fusion.1
  60.2 65.0 %collective-permute-done.3 = bf16[256,2048]{1,0:T(8,128)(2,1)S(1)} collective-permute-done((bf16[256,2048]{1,0:T(8,128)(2,1)S(1)}, bf16[256,2048]{1,0:T(8,128)(2,1)S(1)}, u32[]{:S(2)}, u32[]{:S(2)}) %collective-permute-start.3) | collective-permute-done | bytes 1048608 | tf_op jit(solution)/shard_map/ppermute | solution.py:28
  125.1 0.6 fusion.6
  125.8 5.8 %fusion.37 = bf16[256,1024]{1,0:T(8,128)(2,1)S(1)} fusion(bf16[2,4096,1024]{2,1,0:T(8,128)(2,1)} %all-gather.6.cloned.1.call-done, f32[4096]{0:T(1024)S(1)} %bitcast.128, f32[256]{0:T(256)S(1)} %add_rsqrt_fusion.1, bf16[256,2048]{1,0:T(8,128)(2,1)S(1)} %collective-permute-done.3, bf16[256,2048]{1,0:T(8,128)(2,1)S(1)} %constant_dynamic-slice_fusion, pred[]{:T(512)S(6)} %eq.93), kind=kOutput, calls=%fused_computation.63 | convolution fusion | flops 2161639424 | bytes 11027457 | tf_op jit(solution)/shard_map/dot_general | solution.py:53
  131.6 2.9 gather_fusion.1
  134.5 2.3 collective-permute-start.4
  136.7 19.5 %collective-permute-done.4 = bf16[8,64,896]{2,1,0:T(8,128)(2,1)S(1)} collective-permute-done((bf16[8,64,896]{2,1,0:T(8,128)(2,1)S(1)}, bf16[8,64,896]{2,1,0:T(8,128)(2,1)S(1)}, u32[]{:S(2)}, u32[]{:S(2)}) %collective-permute-start.4) | collective-permute-done | bytes 917536 | tf_op jit(solution)/shard_map/ppermute | solution.py:28
  156.2 0.8 maximum_select_fusion.3
  157.0 2.1 collective-permute-start.5
  159.3 3.3 %collective-permute-done.5 = bf16[8,128,896]{2,1,0:T(8,128)(2,1)} collective-permute-done((bf16[8,128,896]{2,1,0:T(8,128)(2,1)S(1)}, bf16[8,128,896]{2,1,0:T(8,128)(2,1)}, u32[]{:S(2)}, u32[]{:S(2)}) %collective-permute-start.5) | collective-permute-done | bytes 1835040 | tf_op jit(solution)/shard_map/ppermute | solution.py:28
  162.6 3.6 %maximum_select_fusion = bf16[16,128,896]{2,1,0:T(8,128)(2,1)} fusion(bf16[8,128,896]{2,1,0:T(8,128)(2,1)} %collective-permute-done.5, bf16[8,128,896]{2,1,0:T(8,128)(2,1)S(1)} %maximum_select_fusion.3, pred[]{:T(512)S(6)} %eq.92), kind=kLoop, calls=%fused_computation.23 | loop fusion | flops 5505024 | bytes 7340033 | tf_op jit(solution)/shard_map/jit(_where)/select_n | solution.py:34
  166.2 2.9 gather_fusion.2
  169.2 1.3 copy-done.8
  170.4 3.8 %convert_bitcast_fusion.2 = bf16[128,8,8,128]{3,1,2,0:T(8,128)(2,1)S(1)} fusion(bf16[1024,896]{1,0:T(8,128)(2,1)S(1)} %bitcast.117, bf16[2,896,1024]{2,1,0:T(8,128)(2,1)} %all-gather.10.cloned.1.call-done), kind=kOutput, calls=%fused_computation.46 | convolution fusion | flops 1880096768 | bytes 5767168 | tf_op jit(solution)/shard_map/dot_general | solution.py:61
  174.3 0.6 copy.129
  174.9 4.4 %convert_bitcast_fusion.3 = bf16[128,8,8,128]{3,1,2,0:T(8,128)(2,1)S(1)} fusion(bf16[1024,896]{1,0:T(8,128)(2,1)} %bitcast.118, bf16[2,896,1024]{2,1,0:T(8,128)(2,1)} %all-gather.8.cloned.1.call-done), kind=kOutput, calls=%fused_computation.47 | convolution fusion | flops 1880096768 | bytes 5767168 | tf_op jit(solution)/shard_map/dot_general | solution.py:62
  179.3 2.0 copy.130
  181.3 0.8 fusion.20
  182.1 1.4 copy-done.2
  183.5 0.6 fusion.104
  184.1 1.0 copy-done.7
  185.1 5.9 %fusion.49 = bf16[4,64,8,128]{3,1,2,0:T(8,128)(2,1)S(1)} fusion(bf16[4,256,8,128]{3,2,1,0:T(8,128)(2,1)S(1)} %bitcast.116, f32[4,8,64]{2,1,0:T(8,128)S(1)} %fusion.104, f32[4,8,64,256]{3,2,1,0:T(8,128)} %copy-done.2), kind=kOutput, calls=%fused_computation.67 | convolution fusion | flops 136055040 | bytes 4726784 | tf_op jit(solution)/shard_map/chqk,ckhd->cqhd/dot_general | solution.py:71
  191.4 5.7 %fusion.4 = f32[256,4096]{1,0:T(8,128)S(1)} fusion(bf16[2,1024,4096]{2,1,0:T(8,128)(2,1)} %all-gather.12.cloned.1.call-done, bf16[32,8,8,128]{3,2,1,0:T(8,128)(2,1)S(1)} %bitcast.123), kind=kOutput, calls=%fused_computation.10 | convolution fusion | flops 2147483648 | bytes 13107200 | tf_op jit(solution)/shard_map/dot_general | solution.py:75
  197.1 2.0 copy-done.6
  199.3 1.5 collective-permute-start.6
  200.8 22.9 %collective-permute-done.6 = bf16[256,2048]{1,0:T(8,128)(2,1)S(1)} collective-permute-done((bf16[256,2048]{1,0:T(8,128)(2,1)S(1)}, bf16[256,2048]{1,0:T(8,128)(2,1)S(1)}, u32[]{:S(2)}, u32[]{:S(2)}) %collective-permute-start.6) | collective-permute-done | bytes 1048608 | tf_op jit(solution)/shard_map/ppermute | solution.py:28
  223.7 2.3 add_convert_fusion.1
  226.0 1.8 collective-permute-start.7
  227.8 4.0 %convert_bitcast_fusion = bf16[128,8,8,128]{3,1,2,0:T(8,128)(2,1)S(1)} fusion(bf16[1024,896]{1,0:T(8,128)(2,1)S(1)} %bitcast.119, bf16[2,896,1024]{2,1,0:T(8,128)(2,1)} %all-gather.10.cloned.1.call-done), kind=kOutput, calls=%fused_computation.38 | convolution fusion | flops 1880096768 | bytes 5767168 | tf_op jit(solution)/shard_map/dot_general | solution.py:61
  231.8 0.6 copy.133
  232.4 1.4 copy-done.16
  233.8 2.3 convert_bitcast_fusion.1
  236.2 1.9 copy.134
  238.1 11.7 %collective-permute-done.7 = bf16[256,2048]{1,0:T(8,128)(2,1)S(1)} collective-permute-done((bf16[256,2048]{1,0:T(8,128)(2,1)S(1)}, bf16[256,2048]{1,0:T(8,128)(2,1)S(1)}, u32[]{:S(2)}, u32[]{:S(2)}) %collective-permute-start.7) | collective-permute-done | bytes 1048608 | tf_op jit(solution)/shard_map/ppermute | solution.py:28
  249.8 0.6 fusion.9
  250.5 2.5 fusion.52
  253.1 0.8 fusion.16
  254.0 1.3 copy-done.3
  255.3 0.6 fusion.105
  255.9 6.5 %fusion.46 = bf16[4,64,8,128]{3,1,2,0:T(8,128)(2,1)S(1)} fusion(bf16[4,256,8,128]{3,2,1,0:T(8,128)(2,1)} %bitcast.115, f32[4,8,64]{2,1,0:T(8,128)S(1)} %fusion.105, f32[4,8,64,256]{3,2,1,0:T(8,128)} %copy-done.3), kind=kOutput, calls=%fused_computation.66 | convolution fusion | flops 136055040 | bytes 4726784 | tf_op jit(solution)/shard_map/chqk,ckhd->cqhd/dot_general | solution.py:71
  262.8 5.7 %fusion.2 = f32[256,4096]{1,0:T(8,128)S(1)} fusion(bf16[2,1024,4096]{2,1,0:T(8,128)(2,1)} %all-gather.12.cloned.1.call-done, bf16[32,8,8,128]{3,2,1,0:T(8,128)(2,1)S(1)} %bitcast.124), kind=kOutput, calls=%fused_computation.6 | convolution fusion | flops 2147483648 | bytes 13107200 | tf_op jit(solution)/shard_map/dot_general | solution.py:75
  268.7 1.5 collective-permute-start.8
  270.2 21.2 %collective-permute-done.8 = bf16[256,2048]{1,0:T(8,128)(2,1)S(1)} collective-permute-done((bf16[256,2048]{1,0:T(8,128)(2,1)S(1)}, bf16[256,2048]{1,0:T(8,128)(2,1)S(1)}, u32[]{:S(2)}, u32[]{:S(2)}) %collective-permute-start.8) | collective-permute-done | bytes 1048608 | tf_op jit(solution)/shard_map/ppermute | solution.py:28
  291.4 1.5 add_convert_fusion
  (89 shorter events, 5.0 us)
Async XLA Ops:
  6.5 3.9 %copy-start = (bf16[512,896]{1,0:T(8,128)(2,1)S(1)}, bf16[512,896]{1,0:T(8,128)(2,1)}, u32[]{:S(2)}) copy-start(bf16[512,896]{1,0:T(8,128)(2,1)} %param.16) | copy-start | bytes 2752516
  6.5 119.2 %all-gather.6.cloned.1.call-start = ((), (), s32[]{:S(2)}) async-start(), calls=%async_computation.1 | async-start | bytes 25165824 | tf_op jit(solution)/shard_map/all_gather | solution.py:105
  7.3 161.9 %all-gather.10.cloned.1.call-start = ((), (), s32[]{:S(2)}) async-start(), calls=%async_computation.3 | async-start | bytes 5505024 | tf_op jit(solution)/shard_map/all_gather | solution.py:107
  8.0 166.9 %all-gather.8.cloned.1.call-start = ((), (), s32[]{:S(2)}) async-start(), calls=%async_computation.2 | async-start | bytes 5505024 | tf_op jit(solution)/shard_map/all_gather | solution.py:108
  8.7 1.2 copy-start.4
  8.8 1.4 copy-start.12
  8.8 182.6 %all-gather.12.cloned.1.call-start = ((), (), s32[]{:S(2)}) async-start(), calls=%async_computation.4 | async-start | bytes 25165824 | tf_op jit(solution)/shard_map/all_gather | solution.py:109
  10.5 5.3 %copy-start.11 = (s32[256,2]{0,1:T(2,128)S(1)}, s32[256,2]{0,1:T(2,128)}, u32[]{:S(2)}) copy-start(s32[256,2]{0,1:T(2,128)} %param.13) | copy-start | bytes 6148
  14.4 5.1 %collective-permute-start = (f32[512,896]{1,0:T(8,128)}, f32[512,896]{1,0:T(8,128)}, u32[]{:S(2)}, u32[]{:S(2)}) collective-permute-start(f32[512,896]{1,0:T(8,128)} %fusion.67), channel_id=1, source_target_pairs={{0,2},{2,0},{1,3},{3,1},{4,6},{6,4},{5,7},{7,5},{8,10},{10,8},{9,1... | collective-permute-start | bytes 5505032 | tf_op jit(solution)/shard_map/ppermute | solution.py:28
  22.2 1.3 copy-start.5
  23.5 11.9 %collective-permute-start.1 = (f32[4,1,32,896]{3,2,0,1:T(8,128)S(1)}, f32[4,1,32,896]{3,2,0,1:T(8,128)S(1)}, u32[]{:S(2)}, u32[]{:S(2)}) collective-permute-start(f32[4,1,32,896]{3,2,0,1:T(8,128)S(1)} %dynamic-slice_bitcast_fusion), channel_id=1, source_target_pairs={{0,1},{1,0},{2,3},{3,2},{4,5},{5,4},{6,7},{7,6},{8,9},{9,8},{10,11... | collective-permute-start | bytes 1376264 | tf_op jit(solution)/shard_map/ppermute | solution.py:28
  36.6 3.3 %collective-permute-start.2 = (f32[4,1,32,896]{3,2,0,1:T(8,128)S(1)}, f32[4,1,32,896]{3,2,0,1:T(8,128)S(1)}, u32[]{:S(2)}, u32[]{:S(2)}) collective-permute-start(f32[4,1,32,896]{3,2,0,1:T(8,128)S(1)} %bitcast_add_fusion), channel_id=1, source_target_pairs={{0,2},{2,0},{1,3},{3,1},{4,6},{6,4},{5,7},{7,5},{8,10},{10,8},{9,1... | collective-permute-start | bytes 1376264 | tf_op jit(solution)/shard_map/ppermute | solution.py:28
  42.8 88.7 %all-to-all-start = ((bf16[32,64,896]{2,1,0:T(8,128)(2,1)}), bf16[32,64,896]{2,1,0:T(8,128)(2,1)}, u32[]{:S(2)}, u32[]{:S(2)}) async-start(bf16[32,64,896]{2,1,0:T(8,128)(2,1)} %gather_fusion), calls=%async_computation | async-start | bytes 7340032 | tf_op jit(solution)/shard_map/all_to_all | solution.py:141
  54.1 3.1 %copy-start.10 = (f32[1,4096]{1,0:T(1,128)S(1)}, f32[1,4096]{1,0:T(1,128)}, u32[]{:S(2)}) copy-start(f32[1,4096]{1,0:T(1,128)} %param.17) | copy-start | bytes 49156
  55.4 69.7 %collective-permute-start.3 = (bf16[256,2048]{1,0:T(8,128)(2,1)S(1)}, bf16[256,2048]{1,0:T(8,128)(2,1)S(1)}, u32[]{:S(2)}, u32[]{:S(2)}) collective-permute-start(bf16[256,2048]{1,0:T(8,128)(2,1)S(1)} %constant_dynamic-slice_fusion), channel_id=1, source_target_pairs={{0,1},{1,0},{2,3},{3,2},{4,5},{5,4},{6,7},{7,6},{8,9},{9,8},{10,11... | collective-permute-start | bytes 3145736 | tf_op jit(solution)/shard_map/ppermute | solution.py:28
  56.1 1.1 copy-start.13
  134.4 24.7 %copy-start.14 = (s32[16]{0:T(128)S(1)}, s32[16]{0:T(128)}, u32[]{:S(2)}) copy-start(s32[16]{0:T(128)} %copy-done.13) | copy-start | bytes 196
  134.4 24.6 %copy-start.15 = (s32[16]{0:T(128)S(1)}, s32[16]{0:T(128)}, u32[]{:S(2)}) copy-start(s32[16]{0:T(128)} %get-tuple-element.13) | copy-start | bytes 196
  134.5 21.8 %collective-permute-start.4 = (bf16[8,64,896]{2,1,0:T(8,128)(2,1)S(1)}, bf16[8,64,896]{2,1,0:T(8,128)(2,1)S(1)}, u32[]{:S(2)}, u32[]{:S(2)}) collective-permute-start(bf16[8,64,896]{2,1,0:T(8,128)(2,1)S(1)} %gather_fusion.1), channel_id=1, source_target_pairs={{0,1},{1,0},{2,3},{3,2},{4,5},{5,4},{6,7},{7,6},{8,9},{9,8},{10,11... | collective-permute-start | bytes 2752520 | tf_op jit(solution)/shard_map/ppermute | solution.py:28
  157.0 5.6 %collective-permute-start.5 = (bf16[8,128,896]{2,1,0:T(8,128)(2,1)S(1)}, bf16[8,128,896]{2,1,0:T(8,128)(2,1)}, u32[]{:S(2)}, u32[]{:S(2)}) collective-permute-start(bf16[8,128,896]{2,1,0:T(8,128)(2,1)S(1)} %maximum_select_fusion.3), channel_id=1, source_target_pairs={{0,2},{2,0},{1,3},{3,1},{4,6},{6,4},{5,7},{7,5},{8,10},{10,8},{9,1... | collective-permute-start | bytes 5505032 | tf_op jit(solution)/shard_map/ppermute | solution.py:28
  169.1 1.3 copy-start.8
  182.1 1.4 copy-start.2
  183.5 1.6 copy-start.7
  197.1 2.0 copy-start.6
  199.3 24.4 %collective-permute-start.6 = (bf16[256,2048]{1,0:T(8,128)(2,1)S(1)}, bf16[256,2048]{1,0:T(8,128)(2,1)S(1)}, u32[]{:S(2)}, u32[]{:S(2)}) collective-permute-start(bf16[256,2048]{1,0:T(8,128)(2,1)S(1)} %dynamic-slice_convert_fusion.1), channel_id=1, source_target_pairs={{0,1},{1,0},{2,3},{3,2},{4,5},{5,4},{6,7},{7,6},{8,9},{9,8},{10,11... | collective-permute-start | bytes 3145736 | tf_op jit(solution)/shard_map/ppermute | solution.py:28
  200.8 27.0 %copy-start.9 = (bf16[8,128,896]{2,1,0:T(8,128)(2,1)S(1)}, bf16[8,128,896]{2,1,0:T(8,128)(2,1)}, u32[]{:S(2)}) copy-start(bf16[8,128,896]{2,1,0:T(8,128)(2,1)} %copy-done.8) | copy-start | bytes 5505028
  226.0 23.8 %collective-permute-start.7 = (bf16[256,2048]{1,0:T(8,128)(2,1)S(1)}, bf16[256,2048]{1,0:T(8,128)(2,1)S(1)}, u32[]{:S(2)}, u32[]{:S(2)}) collective-permute-start(bf16[256,2048]{1,0:T(8,128)(2,1)S(1)} %add_convert_fusion.1), channel_id=1, source_target_pairs={{0,1},{1,0},{2,3},{3,2},{4,5},{5,4},{6,7},{7,6},{8,9},{9,8},{10,11... | collective-permute-start | bytes 3145736 | tf_op jit(solution)/shard_map/ppermute | solution.py:28
  227.8 22.7 %slice-start = ((s8[16777216]{0:T(1024)(128)(4,1)}), s8[4194304]{0:T(1024)(128)(4,1)S(1)}, s32[]{:S(2)}) async-start(s8[16777216]{0:T(1024)(128)(4,1)} %bitcast.129), calls=%async_computation.5 | async-start | bytes 8388608
  227.8 22.7 %slice-start.1 = ((s8[16777216]{0:T(1024)(128)(4,1)}), s8[4194304]{0:T(1024)(128)(4,1)S(1)}, s32[]{:S(2)}) async-start(s8[16777216]{0:T(1024)(128)(4,1)} %bitcast.129), calls=%async_computation.6 | async-start | bytes 8388608
  231.8 2.0 copy-start.16
  233.8 16.7 %slice-start.2 = ((s8[16777216]{0:T(1024)(128)(4,1)}), s8[4194304]{0:T(1024)(128)(4,1)S(1)}, s32[]{:S(2)}) async-start(s8[16777216]{0:T(1024)(128)(4,1)} %bitcast.129), calls=%async_computation.7 | async-start | bytes 8388608
  233.8 16.7 %slice-start.3 = ((s8[16777216]{0:T(1024)(128)(4,1)}), s8[4194304]{0:T(1024)(128)(4,1)S(1)}, s32[]{:S(2)}) async-start(s8[16777216]{0:T(1024)(128)(4,1)} %bitcast.129), calls=%async_computation.8 | async-start | bytes 8388608
  254.0 1.4 copy-start.3
  268.5 24.4 %copy-start.1 = (bf16[512,896]{1,0:T(8,128)(2,1)S(1)}, bf16[512,896]{1,0:T(8,128)(2,1)}, u32[]{:S(2)}) copy-start(bf16[512,896]{1,0:T(8,128)(2,1)} %param.16) | copy-start | bytes 2752516
  268.7 22.7 %collective-permute-start.8 = (bf16[256,2048]{1,0:T(8,128)(2,1)S(1)}, bf16[256,2048]{1,0:T(8,128)(2,1)S(1)}, u32[]{:S(2)}, u32[]{:S(2)}) collective-permute-start(bf16[256,2048]{1,0:T(8,128)(2,1)S(1)} %dynamic-slice_convert_fusion), channel_id=1, source_target_pairs={{0,1},{1,0},{2,3},{3,2},{4,5},{5,4},{6,7},{7,6},{8,9},{9,8},{10,11... | collective-permute-start | bytes 3145736 | tf_op jit(solution)/shard_map/ppermute | solution.py:28
Sparse Core Ops, SparseCore 0:
  9.0 37.0 all-gather.5
  47.7 16.9 all-gather.9
  66.4 17.0 all-gather.7
  84.9 34.1 all-gather.11

commit v4 on v3

--- a/solution.py
+++ b/solution.py
@@ -46,8 +46,9 @@
     return mine + swap(theirs.astype(link_type), axis).astype(mine.dtype)
 
 
-def layer_queries(state_rows, gain_vec, query_w):
-    whole_rows = pair_gather(state_rows, "mp", 1)
+def layer_queries(state_rows, gain_vec, query_w, whole_rows=None):
+    if whole_rows is None:
+        whole_rows = pair_gather(state_rows, "mp", 1)
     floats = whole_rows.astype(jnp.float32)
     normed = rms_scale(floats, gain_vec).astype(jnp.bfloat16)
     return (jnp.dot(normed, query_w, preferred_element_type=jnp.float32) * HD ** (-0.5)).astype(
@@ -109,7 +110,7 @@
     wo = lax.all_gather(w_out, "section", axis=0, tiled=True)
     micro_tokens = hidden_in.shape[0] // channels
     state = lax.dynamic_slice_in_dim(hidden_in, sec_index * micro_tokens, micro_tokens, 0)
-    queries = layer_queries(state, gains[0], wq[0])
+    first_rows = pair_gather(state, "mp", 1)
 
     held_rows = database.reshape(-1, E).astype(jnp.float32)
     terms = encoder_terms(held_rows, enc_gain, enc_up, enc_down)
@@ -138,6 +139,8 @@
     serve = (owners == db_index) & (channel == sec_index)
     send_local = jnp.sum(jnp.where(serve, within, 0), axis=-1)
     payload = enc_half[send_local]
+    payload, first_rows = lax.optimization_barrier((payload, first_rows))
+    queries = layer_queries(state, gains[0], wq[0], first_rows)
     received = lax.all_to_all(payload, "db", split_axis=0, concat_axis=0, tiled=True)
     received, queries = lax.optimization_barrier((received, queries))
 

time: 302 us -> 291 us (0.964)
  waiting for transfers between devices: 161 us -> 146 us
    ppermute x9, waiting for transfers between devices: 158 us -> 105 us  [swap(): return lax.ppermute(block, axis, [(0, 1), (1, 0)])]
    all_to_all x1, waiting for transfers between devices: 0.01 us -> 38 us  [body(): lax.all_to_all(payload, 'db', split_axis=0, concat_axis=0, tiled=True)]
    select_n x2 -> x3, other arithmetic: 4.36 us -> 6.69 us  [pair_gather(): jnp.where(first, jnp.concatenate([block, other], axis=dim), jnp.concatena...]
    unnamed x49 -> x55, local copies, waits for them, and re-layouts: 15.8 us -> 15.7 us
  transfers between devices with their start and end apart: 14 -> 14, of which waited for: 9 -> 7; matrix products, arithmetic and copies ran while one was open for 20% -> 22% of each run, Pallas kernels for 0% -> 0%
where the time goes in v4:
time: 291 us; the launch traced here: 286 us
  waiting for transfers between devices  146 us (50%)
  matrix products  53.1 us (18%)
  local copies, waits for them, and re-layouts  27.8 us (10%)
  starting transfers between devices  23.5 us (8%)
  other arithmetic  20.1 us (7%)
  between operations  13.8 us (5%)
    ppermute x9, waiting for transfers between devices, swap(): return lax.ppermute(block, axis, [(0, 1), (1, 0)])  105 us
    all_to_all x1, waiting for transfers between devices, body(): lax.all_to_all(payload, 'db', split_axis=0, concat_axis=0, tiled=True)  38 us
    unnamed x55, local copies, waits for them, and re-layouts  15.7 us
    ppermute x9, starting transfers between devices, swap(): return lax.ppermute(block, axis, [(0, 1), (1, 0)])  12.5 us
    dot_general x2, matrix products, cross_layer(): jnp.einsum('chqk,ckhd->cqhd', soft_weights, value_four, preferred_element...  12.4 us
    dot_general x2, matrix products, cross_layer(): partial_out = jnp.dot(context, out_w, preferred_element_type=jnp.float32)  11.4 us
    all_to_all x1, starting transfers between devices, body(): lax.all_to_all(payload, 'db', split_axis=0, concat_axis=0, tiled=True)  10.9 us
    dot_general x2, matrix products, layer_queries(): jnp.dot(normed, query_w, preferred_element_type=jnp.float32) * HD ** (-0.5)  9.22 us
  transfers between devices with their start and end apart: 14, of which 7 were waited for; matrix products, arithmetic and copies ran while one was open for 22% of the time, Pallas kernels for 0%

profile of v4, /device:TPU:1, one launch (start us, length us, event | category | flops | bytes accessed | tf_op | source)
XLA Modules:
  0.0 286.0 jit_solution(12594216521739691701)
XLA Ops:
  6.5 0.7 all-gather.6.cloned.1.call-update
  7.3 0.7 all-gather.10.cloned.1.call-update
  8.1 0.7 all-gather.8.cloned.1.call-update
  8.8 0.5 all-gather.12.cloned.1.call-update
  9.3 0.6 copy-done.4
  10.5 3.8 %fusion.67 = f32[512,896]{1,0:T(8,128)} fusion(bf16[512,896]{1,0:T(8,128)(2,1)S(1)} %copy-done, bf16[512,896]{1,0:T(8,128)(2,1)S(1)} %fusion.27, bf16[896,512]{1,0:T(8,128)(2,1)} %param.15), kind=kOutput, calls=%fused_computation.82 | convolution fusion | flops 941883392 | bytes 4587520 | tf_op jit(solution)/shard_map/dot_general | solution.py:24
  14.3 1.4 collective-permute-start
  15.7 1.3 constant_dynamic-slice_fusion
  17.0 1.4 collective-permute-start.3
  19.8 2.9 %add.170 = f32[512,896]{1,0:T(8,128)S(1)} add(f32[512,896]{1,0:T(8,128)} %fusion.67, f32[512,896]{1,0:T(8,128)} %collective-permute-done) | non-fusion elementwise | flops 458752 | bytes 5505024 | tf_op jit(solution)/shard_map/add | solution.py:117
  22.7 1.2 copy-done.8
  24.0 0.7 collective-permute-start.1
  25.2 26.4 %collective-permute-done.1 = f32[4,1,32,896]{3,2,0,1:T(8,128)S(1)} collective-permute-done((f32[4,1,32,896]{3,2,0,1:T(8,128)S(1)}, f32[4,1,32,896]{3,2,0,1:T(8,128)S(1)}, u32[]{:S(2)}, u32[]{:S(2)}) %collective-permute-start.1) | collective-permute-done | bytes 458784 | tf_op jit(solution)/shard_map/ppermute | solution.py:28
  51.6 1.1 bitcast_add_fusion
  52.7 1.0 collective-permute-start.2
  53.6 2.3 maximum_select_fusion.1
  56.1 2.9 %gather_fusion = bf16[32,64,896]{2,1,0:T(8,128)(2,1)} fusion(bf16[4,64,896]{2,1,0:T(8,128)(2,1)S(1)} %fusion.66, s32[1024]{0:T(1024)S(1)} %pad_clamp_fusion.2), kind=kCustom, calls=%fused_computation | custom fusion | bytes 7340160 | tf_op jit(solution)/shard_map/gather | solution.py:141
  59.0 10.9 %all-to-all-start = ((bf16[32,64,896]{2,1,0:T(8,128)(2,1)}), bf16[32,64,896]{2,1,0:T(8,128)(2,1)}, u32[]{:S(2)}, u32[]{:S(2)}) async-start(bf16[32,64,896]{2,1,0:T(8,128)(2,1)} %gather_fusion), calls=%async_computation | async-start | bytes 7340032 | tf_op jit(solution)/shard_map/all_to_all | solution.py:144
  70.4 0.7 multiply_reduce_fusion.1
  71.2 1.8 all-gather
  73.1 0.6 pad_clamp_fusion.1
  73.7 0.5 fusion.6
  74.3 6.7 %fusion.37 = bf16[256,1024]{1,0:T(8,128)(2,1)S(1)} fusion(bf16[2,4096,1024]{2,1,0:T(8,128)(2,1)} %all-gather.6.cloned.1.call-done, bf16[256,4096]{1,0:T(8,128)(2,1)S(1)} %maximum_select_fusion.1, f32[4096]{0:T(1024)S(1)} %bitcast.128, f32[256]{0:T(256)S(1)} %add_rsqrt_fusion.1), kind=kOutput, calls=%fused_computation.63 | convolution fusion | flops 2152202240 | bytes 11027456 | tf_op jit(solution)/shard_map/dot_general | solution.py:54
  81.0 38.0 %all-to-all-done = bf16[32,64,896]{2,1,0:T(8,128)(2,1)} async-done(((bf16[32,64,896]{2,1,0:T(8,128)(2,1)}), bf16[32,64,896]{2,1,0:T(8,128)(2,1)}, u32[]{:S(2)}, u32[]{:S(2)}) %all-to-all-start) | async-done | bytes 3670048 | tf_op jit(solution)/shard_map/all_to_all | solution.py:144
  118.9 2.9 gather_fusion.1
  121.8 1.4 collective-permute-start.4
  123.3 19.6 %collective-permute-done.4 = bf16[8,64,896]{2,1,0:T(8,128)(2,1)S(1)} collective-permute-done((bf16[8,64,896]{2,1,0:T(8,128)(2,1)S(1)}, bf16[8,64,896]{2,1,0:T(8,128)(2,1)S(1)}, u32[]{:S(2)}, u32[]{:S(2)}) %collective-permute-start.4) | collective-permute-done | bytes 917536 | tf_op jit(solution)/shard_map/ppermute | solution.py:28
  142.9 0.8 maximum_select_fusion.3
  143.6 2.1 collective-permute-start.5
  145.9 3.3 %collective-permute-done.5 = bf16[8,128,896]{2,1,0:T(8,128)(2,1)} collective-permute-done((bf16[8,128,896]{2,1,0:T(8,128)(2,1)S(1)}, bf16[8,128,896]{2,1,0:T(8,128)(2,1)}, u32[]{:S(2)}, u32[]{:S(2)}) %collective-permute-start.5) | collective-permute-done | bytes 1835040 | tf_op jit(solution)/shard_map/ppermute | solution.py:28
  149.3 3.6 %maximum_select_fusion = bf16[16,128,896]{2,1,0:T(8,128)(2,1)} fusion(bf16[8,128,896]{2,1,0:T(8,128)(2,1)} %collective-permute-done.5, bf16[8,128,896]{2,1,0:T(8,128)(2,1)S(1)} %maximum_select_fusion.3, pred[]{:T(512)S(6)} %eq.92), kind=kLoop, calls=%fused_computation.23 | loop fusion | flops 5505024 | bytes 7340033 | tf_op jit(solution)/shard_map/jit(_where)/select_n | solution.py:34
  152.8 2.9 %gather_fusion.2 = bf16[8,128,896]{2,1,0:T(8,128)(2,1)S(1)} fusion(bf16[16,128,896]{2,1,0:T(8,128)(2,1)} %maximum_select_fusion, s32[1024]{0:T(1024)S(1)} %pad_clamp_fusion), kind=kCustom, calls=%fused_computation.2 | custom fusion | bytes 3670048 | tf_op jit(solution)/shard_map/gather | solution.py:159
  155.8 1.3 copy-done.11
  157.0 3.8 %convert_bitcast_fusion.2 = bf16[128,8,8,128]{3,1,2,0:T(8,128)(2,1)S(1)} fusion(bf16[1024,896]{1,0:T(8,128)(2,1)S(1)} %bitcast.117, bf16[2,896,1024]{2,1,0:T(8,128)(2,1)} %all-gather.10.cloned.1.call-done), kind=kOutput, calls=%fused_computation.46 | convolution fusion | flops 1880096768 | bytes 5767168 | tf_op jit(solution)/shard_map/dot_general | solution.py:62
  160.9 0.6 copy.129
  161.5 4.4 %convert_bitcast_fusion.3 = bf16[128,8,8,128]{3,1,2,0:T(8,128)(2,1)S(1)} fusion(bf16[1024,896]{1,0:T(8,128)(2,1)} %bitcast.118, bf16[2,896,1024]{2,1,0:T(8,128)(2,1)} %all-gather.8.cloned.1.call-done), kind=kOutput, calls=%fused_computation.47 | convolution fusion | flops 1880096768 | bytes 5767168 | tf_op jit(solution)/shard_map/dot_general | solution.py:63
  165.9 2.0 copy.130
  167.9 0.8 fusion.20
  168.8 1.4 copy-done.2
  170.1 0.6 fusion.103
  170.8 1.0 copy-done.10
  171.7 5.9 %fusion.49 = bf16[4,64,8,128]{3,1,2,0:T(8,128)(2,1)S(1)} fusion(bf16[4,256,8,128]{3,2,1,0:T(8,128)(2,1)S(1)} %bitcast.116, f32[4,8,64]{2,1,0:T(8,128)S(1)} %fusion.103, f32[4,8,64,256]{3,2,1,0:T(8,128)} %copy-done.2), kind=kOutput, calls=%fused_computation.67 | convolution fusion | flops 136055040 | bytes 4726784 | tf_op jit(solution)/shard_map/chqk,ckhd->cqhd/dot_general | solution.py:72
  178.0 5.7 %fusion.4 = f32[256,4096]{1,0:T(8,128)S(1)} fusion(bf16[2,1024,4096]{2,1,0:T(8,128)(2,1)} %all-gather.12.cloned.1.call-done, bf16[32,8,8,128]{3,2,1,0:T(8,128)(2,1)S(1)} %bitcast.123), kind=kOutput, calls=%fused_computation.10 | convolution fusion | flops 2147483648 | bytes 13107200 | tf_op jit(solution)/shard_map/dot_general | solution.py:76
  183.7 2.0 copy-done.9
  185.9 1.4 collective-permute-start.6
  187.3 23.0 %collective-permute-done.6 = bf16[256,2048]{1,0:T(8,128)(2,1)S(1)} collective-permute-done((bf16[256,2048]{1,0:T(8,128)(2,1)S(1)}, bf16[256,2048]{1,0:T(8,128)(2,1)S(1)}, u32[]{:S(2)}, u32[]{:S(2)}) %collective-permute-start.6) | collective-permute-done | bytes 1048608 | tf_op jit(solution)/shard_map/ppermute | solution.py:28
  210.3 2.3 add_convert_fusion.1
  212.6 1.7 collective-permute-start.7
  214.3 4.0 %convert_bitcast_fusion = bf16[128,8,8,128]{3,1,2,0:T(8,128)(2,1)S(1)} fusion(bf16[1024,896]{1,0:T(8,128)(2,1)S(1)} %bitcast.119, bf16[2,896,1024]{2,1,0:T(8,128)(2,1)} %all-gather.10.cloned.1.call-done), kind=kOutput, calls=%fused_computation.38 | convolution fusion | flops 1880096768 | bytes 5767168 | tf_op jit(solution)/shard_map/dot_general | solution.py:62
  218.3 0.6 copy.133
  218.9 1.4 copy-done.19
  220.3 2.3 convert_bitcast_fusion.1
  222.7 1.9 copy.134
  224.6 11.8 %collective-permute-done.7 = bf16[256,2048]{1,0:T(8,128)(2,1)S(1)} collective-permute-done((bf16[256,2048]{1,0:T(8,128)(2,1)S(1)}, bf16[256,2048]{1,0:T(8,128)(2,1)S(1)}, u32[]{:S(2)}, u32[]{:S(2)}) %collective-permute-start.7) | collective-permute-done | bytes 1048608 | tf_op jit(solution)/shard_map/ppermute | solution.py:28
  236.4 0.6 fusion.9
  237.1 2.5 fusion.52
  239.7 0.8 fusion.16
  240.6 1.3 copy-done.3
  241.9 0.6 fusion.104
  242.5 6.5 %fusion.46 = bf16[4,64,8,128]{3,1,2,0:T(8,128)(2,1)S(1)} fusion(bf16[4,256,8,128]{3,2,1,0:T(8,128)(2,1)} %bitcast.115, f32[4,8,64]{2,1,0:T(8,128)S(1)} %fusion.104, f32[4,8,64,256]{3,2,1,0:T(8,128)} %copy-done.3), kind=kOutput, calls=%fused_computation.66 | convolution fusion | flops 136055040 | bytes 4726784 | tf_op jit(solution)/shard_map/chqk,ckhd->cqhd/dot_general | solution.py:72
  249.4 5.7 %fusion.2 = f32[256,4096]{1,0:T(8,128)S(1)} fusion(bf16[2,1024,4096]{2,1,0:T(8,128)(2,1)} %all-gather.12.cloned.1.call-done, bf16[32,8,8,128]{3,2,1,0:T(8,128)(2,1)S(1)} %bitcast.124), kind=kOutput, calls=%fused_computation.6 | convolution fusion | flops 2147483648 | bytes 13107200 | tf_op jit(solution)/shard_map/dot_general | solution.py:76
  255.3 1.4 collective-permute-start.8
  256.8 21.3 %collective-permute-done.8 = bf16[256,2048]{1,0:T(8,128)(2,1)S(1)} collective-permute-done((bf16[256,2048]{1,0:T(8,128)(2,1)S(1)}, bf16[256,2048]{1,0:T(8,128)(2,1)S(1)}, u32[]{:S(2)}, u32[]{:S(2)}) %collective-permute-start.8) | collective-permute-done | bytes 1048608 | tf_op jit(solution)/shard_map/ppermute | solution.py:28
  278.0 1.5 add_convert_fusion
  (96 shorter events, 4.7 us)
Async XLA Ops:
  6.5 4.0 %copy-start = (bf16[512,896]{1,0:T(8,128)(2,1)S(1)}, bf16[512,896]{1,0:T(8,128)(2,1)}, u32[]{:S(2)}) copy-start(bf16[512,896]{1,0:T(8,128)(2,1)} %param.16) | copy-start | bytes 2752516
  6.5 67.7 %all-gather.6.cloned.1.call-start = ((), (), s32[]{:S(2)}) async-start(), calls=%async_computation.1 | async-start | bytes 25165824 | tf_op jit(solution)/shard_map/all_gather | solution.py:106
  7.3 148.5 %all-gather.10.cloned.1.call-start = ((), (), s32[]{:S(2)}) async-start(), calls=%async_computation.3 | async-start | bytes 5505024 | tf_op jit(solution)/shard_map/all_gather | solution.py:108
  8.0 153.5 %all-gather.8.cloned.1.call-start = ((), (), s32[]{:S(2)}) async-start(), calls=%async_computation.2 | async-start | bytes 5505024 | tf_op jit(solution)/shard_map/all_gather | solution.py:109
  8.7 1.2 copy-start.4
  8.8 1.4 copy-start.15
  8.8 169.2 %all-gather.12.cloned.1.call-start = ((), (), s32[]{:S(2)}) async-start(), calls=%async_computation.4 | async-start | bytes 25165824 | tf_op jit(solution)/shard_map/all_gather | solution.py:110
  14.3 4.1 %copy-start.14 = (s32[256,2]{0,1:T(2,128)S(1)}, s32[256,2]{0,1:T(2,128)}, u32[]{:S(2)}) copy-start(s32[256,2]{0,1:T(2,128)} %param.13) | copy-start | bytes 6148
  14.3 5.5 %collective-permute-start = (f32[512,896]{1,0:T(8,128)}, f32[512,896]{1,0:T(8,128)}, u32[]{:S(2)}, u32[]{:S(2)}) collective-permute-start(f32[512,896]{1,0:T(8,128)} %fusion.67), channel_id=1, source_target_pairs={{0,2},{2,0},{1,3},{3,1},{4,6},{6,4},{5,7},{7,5},{8,10},{10,8},{9,1... | collective-permute-start | bytes 5505032 | tf_op jit(solution)/shard_map/ppermute | solution.py:28
  17.0 5.7 %copy-start.6 = (bf16[256,2048]{1,0:T(8,128)(2,1)}, bf16[256,2048]{1,0:T(8,128)(2,1)S(1)}, u32[]{:S(2)}) copy-start(bf16[256,2048]{1,0:T(8,128)(2,1)S(1)} %constant_dynamic-slice_fusion) | copy-start | bytes 3145732
  17.0 36.7 %collective-permute-start.3 = (bf16[256,2048]{1,0:T(8,128)(2,1)S(1)}, bf16[256,2048]{1,0:T(8,128)(2,1)}, u32[]{:S(2)}, u32[]{:S(2)}) collective-permute-start(bf16[256,2048]{1,0:T(8,128)(2,1)S(1)} %constant_dynamic-slice_fusion), channel_id=1, source_target_pairs={{0,1},{1,0},{2,3},{3,2},{4,5},{5,4},{6,7},{7,6},{8,9},{9,8},{10,11... | collective-permute-start | bytes 3145736 | tf_op jit(solution)/shard_map/ppermute | solution.py:28
  22.7 1.3 copy-start.8
  24.0 27.6 %collective-permute-start.1 = (f32[4,1,32,896]{3,2,0,1:T(8,128)S(1)}, f32[4,1,32,896]{3,2,0,1:T(8,128)S(1)}, u32[]{:S(2)}, u32[]{:S(2)}) collective-permute-start(f32[4,1,32,896]{3,2,0,1:T(8,128)S(1)} %dynamic-slice_bitcast_fusion), channel_id=1, source_target_pairs={{0,1},{1,0},{2,3},{3,2},{4,5},{5,4},{6,7},{7,6},{8,9},{9,8},{10,11... | collective-permute-start | bytes 1376264 | tf_op jit(solution)/shard_map/ppermute | solution.py:28
  25.2 28.5 %copy-start.7 = (bf16[256,2048]{1,0:T(8,128)(2,1)S(1)}, bf16[256,2048]{1,0:T(8,128)(2,1)}, u32[]{:S(2)}) copy-start(bf16[256,2048]{1,0:T(8,128)(2,1)} %copy-done.6) | copy-start | bytes 3145732
  52.7 3.3 %copy-start.5 = (bf16[4,128,896]{2,1,0:T(8,128)(2,1)S(1)}, bf16[4,128,896]{2,1,0:T(8,128)(2,1)}, u32[]{:S(2)}) copy-start(bf16[4,128,896]{2,1,0:T(8,128)(2,1)} %param.12) | copy-start | bytes 2752516
  52.7 3.3 %collective-permute-start.2 = (f32[4,1,32,896]{3,2,0,1:T(8,128)S(1)}, f32[4,1,32,896]{3,2,0,1:T(8,128)S(1)}, u32[]{:S(2)}, u32[]{:S(2)}) collective-permute-start(f32[4,1,32,896]{3,2,0,1:T(8,128)S(1)} %bitcast_add_fusion), channel_id=1, source_target_pairs={{0,2},{2,0},{1,3},{3,1},{4,6},{6,4},{5,7},{7,5},{8,10},{10,8},{9,1... | collective-permute-start | bytes 1376264 | tf_op jit(solution)/shard_map/ppermute | solution.py:28
  59.0 12.1 %copy-start.13 = (f32[1,4096]{1,0:T(1,128)S(1)}, f32[1,4096]{1,0:T(1,128)}, u32[]{:S(2)}) copy-start(f32[1,4096]{1,0:T(1,128)} %param.17) | copy-start | bytes 49156
  59.0 59.9 %all-to-all-start = ((bf16[32,64,896]{2,1,0:T(8,128)(2,1)}), bf16[32,64,896]{2,1,0:T(8,128)(2,1)}, u32[]{:S(2)}, u32[]{:S(2)}) async-start(bf16[32,64,896]{2,1,0:T(8,128)(2,1)} %gather_fusion), calls=%async_computation | async-start | bytes 7340032 | tf_op jit(solution)/shard_map/all_to_all | solution.py:144
  70.2 10.8 %copy-start.16 = (s32[16]{0:T(128)}, s32[16]{0:T(128)S(1)}, u32[]{:S(2)}) copy-start(s32[16]{0:T(128)S(1)} %dynamic-slice_reduce_fusion.1) | copy-start | bytes 196
  121.8 23.9 %copy-start.17 = (s32[16]{0:T(128)S(1)}, s32[16]{0:T(128)}, u32[]{:S(2)}) copy-start(s32[16]{0:T(128)} %copy-done.16) | copy-start | bytes 196
  121.8 23.9 %copy-start.18 = (s32[16]{0:T(128)S(1)}, s32[16]{0:T(128)}, u32[]{:S(2)}) copy-start(s32[16]{0:T(128)} %get-tuple-element.17) | copy-start | bytes 196
  121.8 21.0 %collective-permute-start.4 = (bf16[8,64,896]{2,1,0:T(8,128)(2,1)S(1)}, bf16[8,64,896]{2,1,0:T(8,128)(2,1)S(1)}, u32[]{:S(2)}, u32[]{:S(2)}) collective-permute-start(bf16[8,64,896]{2,1,0:T(8,128)(2,1)S(1)} %gather_fusion.1), channel_id=1, source_target_pairs={{0,1},{1,0},{2,3},{3,2},{4,5},{5,4},{6,7},{7,6},{8,9},{9,8},{10,11... | collective-permute-start | bytes 2752520 | tf_op jit(solution)/shard_map/ppermute | solution.py:28
  143.6 5.6 %collective-permute-start.5 = (bf16[8,128,896]{2,1,0:T(8,128)(2,1)S(1)}, bf16[8,128,896]{2,1,0:T(8,128)(2,1)}, u32[]{:S(2)}, u32[]{:S(2)}) collective-permute-start(bf16[8,128,896]{2,1,0:T(8,128)(2,1)S(1)} %maximum_select_fusion.3), channel_id=1, source_target_pairs={{0,2},{2,0},{1,3},{3,1},{4,6},{6,4},{5,7},{7,5},{8,10},{10,8},{9,1... | collective-permute-start | bytes 5505032 | tf_op jit(solution)/shard_map/ppermute | solution.py:28
  155.7 1.3 copy-start.11
  168.8 1.4 copy-start.2
  170.1 1.6 copy-start.10
  183.7 2.0 copy-start.9
  185.9 24.4 %collective-permute-start.6 = (bf16[256,2048]{1,0:T(8,128)(2,1)S(1)}, bf16[256,2048]{1,0:T(8,128)(2,1)S(1)}, u32[]{:S(2)}, u32[]{:S(2)}) collective-permute-start(bf16[256,2048]{1,0:T(8,128)(2,1)S(1)} %dynamic-slice_convert_fusion.1), channel_id=1, source_target_pairs={{0,1},{1,0},{2,3},{3,2},{4,5},{5,4},{6,7},{7,6},{8,9},{9,8},{10,11... | collective-permute-start | bytes 3145736 | tf_op jit(solution)/shard_map/ppermute | solution.py:28
  187.3 27.0 %copy-start.12 = (bf16[8,128,896]{2,1,0:T(8,128)(2,1)S(1)}, bf16[8,128,896]{2,1,0:T(8,128)(2,1)}, u32[]{:S(2)}) copy-start(bf16[8,128,896]{2,1,0:T(8,128)(2,1)} %copy-done.11) | copy-start | bytes 5505028
  212.6 23.8 %collective-permute-start.7 = (bf16[256,2048]{1,0:T(8,128)(2,1)S(1)}, bf16[256,2048]{1,0:T(8,128)(2,1)S(1)}, u32[]{:S(2)}, u32[]{:S(2)}) collective-permute-start(bf16[256,2048]{1,0:T(8,128)(2,1)S(1)} %add_convert_fusion.1), channel_id=1, source_target_pairs={{0,1},{1,0},{2,3},{3,2},{4,5},{5,4},{6,7},{7,6},{8,9},{9,8},{10,11... | collective-permute-start | bytes 3145736 | tf_op jit(solution)/shard_map/ppermute | solution.py:28
  214.3 22.8 %slice-start = ((s8[16777216]{0:T(1024)(128)(4,1)}), s8[4194304]{0:T(1024)(128)(4,1)S(1)}, s32[]{:S(2)}) async-start(s8[16777216]{0:T(1024)(128)(4,1)} %bitcast.129), calls=%async_computation.5 | async-start | bytes 8388608
  214.3 22.8 %slice-start.1 = ((s8[16777216]{0:T(1024)(128)(4,1)}), s8[4194304]{0:T(1024)(128)(4,1)S(1)}, s32[]{:S(2)}) async-start(s8[16777216]{0:T(1024)(128)(4,1)} %bitcast.129), calls=%async_computation.6 | async-start | bytes 8388608
  218.3 2.0 copy-start.19
  220.3 16.8 %slice-start.2 = ((s8[16777216]{0:T(1024)(128)(4,1)}), s8[4194304]{0:T(1024)(128)(4,1)S(1)}, s32[]{:S(2)}) async-start(s8[16777216]{0:T(1024)(128)(4,1)} %bitcast.129), calls=%async_computation.7 | async-start | bytes 8388608
  220.3 16.8 %slice-start.3 = ((s8[16777216]{0:T(1024)(128)(4,1)}), s8[4194304]{0:T(1024)(128)(4,1)S(1)}, s32[]{:S(2)}) async-start(s8[16777216]{0:T(1024)(128)(4,1)} %bitcast.129), calls=%async_computation.8 | async-start | bytes 8388608
  240.6 1.4 copy-start.3
  255.1 24.4 %copy-start.1 = (bf16[512,896]{1,0:T(8,128)(2,1)S(1)}, bf16[512,896]{1,0:T(8,128)(2,1)}, u32[]{:S(2)}) copy-start(bf16[512,896]{1,0:T(8,128)(2,1)} %param.16) | copy-start | bytes 2752516
  255.3 22.7 %collective-permute-start.8 = (bf16[256,2048]{1,0:T(8,128)(2,1)S(1)}, bf16[256,2048]{1,0:T(8,128)(2,1)S(1)}, u32[]{:S(2)}, u32[]{:S(2)}) collective-permute-start(bf16[256,2048]{1,0:T(8,128)(2,1)S(1)} %dynamic-slice_convert_fusion), channel_id=1, source_target_pairs={{0,1},{1,0},{2,3},{3,2},{4,5},{5,4},{6,7},{7,6},{8,9},{9,8},{10,11... | collective-permute-start | bytes 3145736 | tf_op jit(solution)/shard_map/ppermute | solution.py:28
Sparse Core Ops, SparseCore 0:
  9.0 36.3 all-gather.5
  47.1 16.9 all-gather.9
  65.7 16.9 all-gather.7
  84.2 34.1 all-gather.11

commit v5 on v4

--- a/solution.py
+++ b/solution.py
@@ -159,13 +159,28 @@
     neighbours = all_blocks[mine]
     enc_blocks = neighbours.reshape(-1, NEIGH * NBLOCK, E)
 
+    batches = 2
+    batch_tokens = micro_tokens // batches
+    batch_blocks = enc_blocks.shape[0] // batches
+    states = [state[i * batch_tokens : (i + 1) * batch_tokens] for i in range(batches)]
+    batch_queries = [queries[i * batch_tokens : (i + 1) * batch_tokens] for i in range(batches)]
+    batch_neighbours = [
+        enc_blocks[i * batch_blocks : (i + 1) * batch_blocks] for i in range(batches)
+    ]
     for layer_id in range(wq.shape[0]):
-        if layer_id > 0:
-            queries = layer_queries(state, gains[layer_id], wq[layer_id])
-        state = cross_layer(
-            state, queries, enc_blocks, wq[layer_id], wk[layer_id], wv[layer_id], wo[layer_id]
-        )
-    return state
+        for i in range(batches):
+            if layer_id > 0:
+                batch_queries[i] = layer_queries(states[i], gains[layer_id], wq[layer_id])
+            states[i] = cross_layer(
+                states[i],
+                batch_queries[i],
+                batch_neighbours[i],
+                wq[layer_id],
+                wk[layer_id],
+                wv[layer_id],
+                wo[layer_id],
+            )
+    return jnp.concatenate(states, axis=0)
 
 
 def solution(mesh):

time: 291 us -> 292 us (level)
  the two profiles are of different devices: /device:TPU:1 before, /device:TPU:60 now
where the time goes in v5:
time: 292 us; the launch traced here: 287 us
  waiting for transfers between devices  128 us (44%)
  matrix products  65.5 us (22%)
  starting transfers between devices  34.6 us (12%)
  local copies, waits for them, and re-layouts  25.1 us (9%)
  other arithmetic  17.9 us (6%)
  between operations  14.2 us (5%)
    ppermute x12, waiting for transfers between devices, swap(): return lax.ppermute(block, axis, [(0, 1), (1, 0)])  84.6 us
    all_to_all x1, waiting for transfers between devices, body(): lax.all_to_all(payload, 'db', split_axis=0, concat_axis=0, tiled=True)  40.6 us
    ppermute x12, starting transfers between devices, swap(): return lax.ppermute(block, axis, [(0, 1), (1, 0)])  24 us
    dot_general x4, matrix products, cross_layer(): partial_out = jnp.dot(context, out_w, preferred_element_type=jnp.float32)  18.7 us
    dot_general x3, matrix products, layer_queries(): jnp.dot(normed, query_w, preferred_element_type=jnp.float32) * HD ** (-0.5)  13.5 us
    dot_general x4, matrix products, cross_layer(): jnp.einsum('chqk,ckhd->cqhd', soft_weights, value_four, preferred_element...  12.4 us
    unnamed x64, local copies, waits for them, and re-layouts  10.8 us
    all_to_all x1, starting transfers between devices, body(): lax.all_to_all(payload, 'db', split_axis=0, concat_axis=0, tiled=True)  10.4 us
  transfers between devices with their start and end apart: 17, of which 10 were waited for; matrix products, arithmetic and copies ran while one was open for 28% of the time, Pallas kernels for 0%

profile of v5, /device:TPU:60, one launch (start us, length us, event | category | flops | bytes accessed | tf_op | source)
XLA Modules:
  0.0 286.9 jit_solution(3907985191844124496)
XLA Ops:
  6.5 0.7 all-gather.6.cloned.1.call-update
  7.3 0.7 all-gather.10.cloned.1.call-update
  8.1 0.7 all-gather.8.cloned.1.call-update
  8.8 0.5 all-gather.12.cloned.1.call-update
  9.3 0.6 copy-done.2
  10.5 3.9 %fusion.101 = f32[512,896]{1,0:T(8,128)} fusion(bf16[512,896]{1,0:T(8,128)(2,1)S(1)} %copy-done, bf16[512,896]{1,0:T(8,128)(2,1)S(1)} %fusion.24, bf16[896,512]{1,0:T(8,128)(2,1)} %param.15), kind=kOutput, calls=%fused_computation.137 | convolution fusion | flops 941883392 | bytes 4587520 | tf_op jit(solution)/shard_map/dot_general | solution.py:24
  14.4 1.3 constant_dynamic-slice_fusion
  15.7 1.3 collective-permute-start.3
  18.5 3.1 %add.197 = f32[512,896]{1,0:T(8,128)S(1)} add(f32[512,896]{1,0:T(8,128)} %fusion.101, f32[512,896]{1,0:T(8,128)} %collective-permute-done) | non-fusion elementwise | flops 458752 | bytes 5505024 | tf_op jit(solution)/shard_map/add | solution.py:117
  21.6 1.4 copy-done.8
  23.0 1.3 collective-permute-start.1
  24.8 26.3 %collective-permute-done.1 = f32[4,1,32,896]{3,2,0,1:T(8,128)S(1)} collective-permute-done((f32[4,1,32,896]{3,2,0,1:T(8,128)S(1)}, f32[4,1,32,896]{3,2,0,1:T(8,128)S(1)}, u32[]{:S(2)}, u32[]{:S(2)}) %collective-permute-start.1) | collective-permute-done | bytes 458784 | tf_op jit(solution)/shard_map/ppermute | solution.py:28
  51.1 1.1 bitcast_add_fusion
  52.3 2.4 maximum_select_fusion.1
  54.9 2.9 %gather_fusion = bf16[32,64,896]{2,1,0:T(8,128)(2,1)} fusion(bf16[4,64,896]{2,1,0:T(8,128)(2,1)S(1)} %fusion.100, s32[1024]{0:T(1024)S(1)} %pad_clamp_fusion.2), kind=kCustom, calls=%fused_computation | custom fusion | bytes 7340160 | tf_op jit(solution)/shard_map/gather | solution.py:141
  57.8 10.4 %all-to-all-start = ((bf16[32,64,896]{2,1,0:T(8,128)(2,1)}), bf16[32,64,896]{2,1,0:T(8,128)(2,1)}, u32[]{:S(2)}, u32[]{:S(2)}) async-start(bf16[32,64,896]{2,1,0:T(8,128)(2,1)} %gather_fusion), calls=%async_computation | async-start | bytes 7340032 | tf_op jit(solution)/shard_map/all_to_all | solution.py:144
  69.0 1.8 all-gather
  70.9 0.6 fusion.150
  71.5 0.5 fusion.11
  72.1 6.4 %fusion.60 = bf16[256,1024]{1,0:T(8,128)(2,1)S(1)} fusion(bf16[2,4096,1024]{2,1,0:T(8,128)(2,1)} %all-gather.6.cloned.1.call-done, bf16[256,4096]{1,0:T(8,128)(2,1)S(1)} %maximum_select_fusion.1, f32[4096]{0:T(1024)S(1)} %bitcast.233, f32[256]{0:T(256)S(1)} %add_rsqrt_fusion), kind=kOutput, calls=%fused_computation.80 | convolution fusion | flops 2152202240 | bytes 11027456 | tf_op jit(solution)/shard_map/dot_general | solution.py:54
  78.5 40.6 %all-to-all-done = bf16[32,64,896]{2,1,0:T(8,128)(2,1)} async-done(((bf16[32,64,896]{2,1,0:T(8,128)(2,1)}), bf16[32,64,896]{2,1,0:T(8,128)(2,1)}, u32[]{:S(2)}, u32[]{:S(2)}) %all-to-all-start) | async-done | bytes 3670048 | tf_op jit(solution)/shard_map/all_to_all | solution.py:144
  119.1 2.7 gather_fusion.1
  121.8 3.0 %collective-permute-start.4 = (bf16[8,64,896]{2,1,0:T(8,128)(2,1)S(1)}, bf16[8,64,896]{2,1,0:T(8,128)(2,1)S(1)}, u32[]{:S(2)}, u32[]{:S(2)}) collective-permute-start(bf16[8,64,896]{2,1,0:T(8,128)(2,1)S(1)} %gather_fusion.1), channel_id=1, source_target_pairs={{0,1},{1,0},{2,3},{3,2},{4,5},{5,4},{6,7},{7,6},{8,9},{9,8},{10,11... | collective-permute-start | bytes 2752520 | tf_op jit(solution)/shard_map/ppermute | solution.py:28
  124.8 20.1 %collective-permute-done.4 = bf16[8,64,896]{2,1,0:T(8,128)(2,1)S(1)} collective-permute-done((bf16[8,64,896]{2,1,0:T(8,128)(2,1)S(1)}, bf16[8,64,896]{2,1,0:T(8,128)(2,1)S(1)}, u32[]{:S(2)}, u32[]{:S(2)}) %collective-permute-start.4) | collective-permute-done | bytes 917536 | tf_op jit(solution)/shard_map/ppermute | solution.py:28
  144.9 0.8 maximum_select_fusion.2
  146.5 3.5 %collective-permute-done.5 = bf16[8,128,896]{2,1,0:T(8,128)(2,1)} collective-permute-done((bf16[8,128,896]{2,1,0:T(8,128)(2,1)S(1)}, bf16[8,128,896]{2,1,0:T(8,128)(2,1)}, u32[]{:S(2)}, u32[]{:S(2)}) %collective-permute-start.5) | collective-permute-done | bytes 1835040 | tf_op jit(solution)/shard_map/ppermute | solution.py:28
  149.9 3.7 %maximum_select_fusion = bf16[16,128,896]{2,1,0:T(8,128)(2,1)} fusion(bf16[8,128,896]{2,1,0:T(8,128)(2,1)} %collective-permute-done.5, bf16[8,128,896]{2,1,0:T(8,128)(2,1)S(1)} %maximum_select_fusion.2, pred[]{:T(512)S(6)} %eq.93), kind=kLoop, calls=%fused_computation.23 | loop fusion | flops 5505024 | bytes 7340033 | tf_op jit(solution)/shard_map/jit(_where)/select_n | solution.py:34
  153.6 2.9 %gather_fusion.2 = bf16[8,128,896]{2,1,0:T(8,128)(2,1)S(1)} fusion(bf16[16,128,896]{2,1,0:T(8,128)(2,1)} %maximum_select_fusion, s32[1024]{0:T(1024)S(1)} %pad_clamp_fusion), kind=kCustom, calls=%fused_computation.2 | custom fusion | bytes 3670048 | tf_op jit(solution)/shard_map/gather | solution.py:159
  156.5 1.5 fusion.149
  158.0 3.0 %fusion.49 = bf16[64,8,8,128]{3,1,2,0:T(8,128)(2,1)S(1)} fusion(bf16[512,896]{1,0:T(8,128)(2,1)} %bitcast.221, bf16[2,896,1024]{2,1,0:T(8,128)(2,1)} %all-gather.10.cloned.1.call-done), kind=kOutput, calls=%fused_computation.71 | convolution fusion | flops 940048384 | bytes 3801088 | tf_op jit(solution)/shard_map/dot_general | solution.py:62
  161.4 0.9 copy-done.12
  162.2 2.7 fusion.51
  165.0 1.2 copy.180
  167.1 3.2 %fusion.69 = bf16[2,64,8,128]{3,1,2,0:T(8,128)(2,1)S(1)} fusion(bf16[2,256,8,128]{3,2,1,0:T(8,128)(2,1)} %bitcast.215, f32[2,8,64]{2,1,0:T(8,128)S(1)} %fusion.152, f32[2,8,64,256]{3,2,1,0:T(8,128)S(1)} %fusion.87), kind=kOutput, calls=%fused_computation.91 | convolution fusion | flops 68027648 | bytes 2363392 | tf_op jit(solution)/shard_map/chqk,ckhd->cqhd/dot_general | solution.py:72
  170.4 2.9 %fusion.50 = bf16[64,8,8,128]{3,1,2,0:T(8,128)(2,1)S(1)} fusion(bf16[512,896]{1,0:T(8,128)(2,1)S(1)} %bitcast.217, bf16[2,896,1024]{2,1,0:T(8,128)(2,1)} %all-gather.10.cloned.1.call-done), kind=kOutput, calls=%fused_computation.72 | convolution fusion | flops 940048384 | bytes 3801088 | tf_op jit(solution)/shard_map/dot_general | solution.py:62
  173.6 1.3 fusion.52
  176.0 1.9 fusion.67
  178.1 4.6 %fusion.6 = f32[128,4096]{1,0:T(8,128)S(1)} fusion(bf16[2,1024,4096]{2,1,0:T(8,128)(2,1)} %all-gather.12.cloned.1.call-done, bf16[16,8,8,128]{3,2,1,0:T(8,128)(2,1)S(1)} %bitcast.228), kind=kOutput, calls=%fused_computation.13 | convolution fusion | flops 1073741824 | bytes 10747904 | tf_op jit(solution)/shard_map/dot_general | solution.py:76
  182.8 1.8 collective-permute-start.6
  184.6 4.8 %fusion.5 = f32[128,4096]{1,0:T(8,128)S(1)} fusion(bf16[2,1024,4096]{2,1,0:T(8,128)(2,1)} %all-gather.12.cloned.1.call-done, bf16[16,8,8,128]{3,2,1,0:T(8,128)(2,1)S(1)} %bitcast.227), kind=kOutput, calls=%fused_computation.12 | convolution fusion | flops 1073741824 | bytes 10747904 | tf_op jit(solution)/shard_map/dot_general | solution.py:76
  189.5 11.9 %collective-permute-start.9 = (bf16[128,2048]{1,0:T(8,128)(2,1)S(1)}, bf16[128,2048]{1,0:T(8,128)(2,1)S(1)}, u32[]{:S(2)}, u32[]{:S(2)}) collective-permute-start(bf16[128,2048]{1,0:T(8,128)(2,1)S(1)} %dynamic-slice_convert_fusion.1), channel_id=1, source_target_pairs={{0,1},{1,0},{2,3},{3,2},{4,5},{5,4},{6,7},{7,6},{8,9},{9,8},{10,11... | collective-permute-start | bytes 1572872 | tf_op jit(solution)/shard_map/ppermute | solution.py:28
  201.5 1.3 fusion.53
  203.5 1.3 fusion.55
  204.8 1.2 copy.184
  206.1 8.8 %collective-permute-done.9 = bf16[128,2048]{1,0:T(8,128)(2,1)S(1)} collective-permute-done((bf16[128,2048]{1,0:T(8,128)(2,1)S(1)}, bf16[128,2048]{1,0:T(8,128)(2,1)S(1)}, u32[]{:S(2)}, u32[]{:S(2)}) %collective-permute-start.9) | collective-permute-done | bytes 524320 | tf_op jit(solution)/shard_map/ppermute | solution.py:28
  214.9 0.5 add_convert_fusion.3
  215.8 1.3 fusion.54
  217.3 1.3 fusion.56
  218.6 1.3 copy.176
  219.9 1.7 collective-permute-start.10
  221.6 8.7 %collective-permute-done.7 = bf16[128,2048]{1,0:T(8,128)(2,1)S(1)} collective-permute-done((bf16[128,2048]{1,0:T(8,128)(2,1)S(1)}, bf16[128,2048]{1,0:T(8,128)(2,1)S(1)}, u32[]{:S(2)}, u32[]{:S(2)}) %collective-permute-start.7) | collective-permute-done | bytes 524320 | tf_op jit(solution)/shard_map/ppermute | solution.py:28
  230.8 2.0 fusion.71
  233.3 1.0 copy-done.6
  234.7 3.7 %fusion.68 = bf16[2,64,8,128]{3,1,2,0:T(8,128)(2,1)S(1)} fusion(bf16[2,256,8,128]{3,2,1,0:T(8,128)(2,1)} %bitcast.214, f32[2,8,64]{2,1,0:T(8,128)S(1)} %fusion.154, f32[2,8,64,256]{3,2,1,0:T(8,128)} %copy-done.6), kind=kOutput, calls=%fused_computation.90 | convolution fusion | flops 68027648 | bytes 2363392 | tf_op jit(solution)/shard_map/chqk,ckhd->cqhd/dot_general | solution.py:72
  238.6 1.0 collective-permute-done.10
  240.0 5.1 %fusion.72 = bf16[16,8,8,128]{3,1,2,0:T(8,128)(2,1)S(1)} fusion(bf16[2,4096,1024]{2,1,0:T(8,128)(2,1)} %all-gather.6.cloned.1.call-done, f32[128]{0:T(128)S(1)} %add_rsqrt_fusion.1, f32[4096]{0:T(1024)S(1)} %bitcast.232, bf16[128,2048]{1,0:T(8,128)(2,1)S(1)} %collective-permute-done.10, bf16[128,2048]{1,0:T(8,128)(2,1)S(1)} %get-tuple-element.16, pred[]{:T(512)S(6)} %eq.94), kind=kOutput, calls=%fused_computation.94 | convolution fusion | flops 1080819712 | bytes 9716225 | tf_op jit(solution)/shard_map/dot_general | solution.py:54
  245.6 1.0 copy-done.7
  247.0 3.7 %fusion.70 = bf16[2,64,8,128]{3,1,2,0:T(8,128)(2,1)S(1)} fusion(bf16[2,256,8,128]{3,2,1,0:T(8,128)(2,1)} %bitcast.213, f32[2,8,64]{2,1,0:T(8,128)S(1)} %fusion.153, f32[2,8,64,256]{3,2,1,0:T(8,128)} %copy-done.7), kind=kOutput, calls=%fused_computation.92 | convolution fusion | flops 68027648 | bytes 2363392 | tf_op jit(solution)/shard_map/chqk,ckhd->cqhd/dot_general | solution.py:72
  250.9 4.6 %fusion.9 = f32[128,4096]{1,0:T(8,128)S(1)} fusion(bf16[2,1024,4096]{2,1,0:T(8,128)(2,1)} %all-gather.12.cloned.1.call-done, bf16[16,8,8,128]{3,2,1,0:T(8,128)(2,1)S(1)} %bitcast.229), kind=kOutput, calls=%fused_computation.16 | convolution fusion | flops 1073741824 | bytes 10747904 | tf_op jit(solution)/shard_map/dot_general | solution.py:76
  256.0 4.6 %fusion.10 = f32[128,4096]{1,0:T(8,128)S(1)} fusion(bf16[2,1024,4096]{2,1,0:T(8,128)(2,1)} %all-gather.12.cloned.1.call-done, bf16[16,8,8,128]{3,2,1,0:T(8,128)(2,1)S(1)} %bitcast.226), kind=kOutput, calls=%fused_computation.17 | convolution fusion | flops 1073741824 | bytes 10747904 | tf_op jit(solution)/shard_map/dot_general | solution.py:76
  260.7 1.8 collective-permute-start.8
  262.5 8.0 %collective-permute-done.11 = bf16[128,2048]{1,0:T(8,128)(2,1)S(1)} collective-permute-done((bf16[128,2048]{1,0:T(8,128)(2,1)S(1)}, bf16[128,2048]{1,0:T(8,128)(2,1)S(1)}, u32[]{:S(2)}, u32[]{:S(2)}) %collective-permute-start.11) | collective-permute-done | bytes 524320 | tf_op jit(solution)/shard_map/ppermute | solution.py:28
  270.7 8.2 %collective-permute-done.8 = bf16[128,2048]{1,0:T(8,128)(2,1)S(1)} collective-permute-done((bf16[128,2048]{1,0:T(8,128)(2,1)S(1)}, bf16[128,2048]{1,0:T(8,128)(2,1)S(1)}, u32[]{:S(2)}, u32[]{:S(2)}) %collective-permute-start.8) | collective-permute-done | bytes 524320 | tf_op jit(solution)/shard_map/ppermute | solution.py:28
  279.1 1.1 pad_maximum_fusion
  (134 shorter events, 12.9 us)
Async XLA Ops:
  6.5 4.0 %copy-start = (bf16[512,896]{1,0:T(8,128)(2,1)S(1)}, bf16[512,896]{1,0:T(8,128)(2,1)}, u32[]{:S(2)}) copy-start(bf16[512,896]{1,0:T(8,128)(2,1)} %param.16) | copy-start | bytes 2752516
  6.5 65.5 %all-gather.6.cloned.1.call-start = ((), (), s32[]{:S(2)}) async-start(), calls=%async_computation.1 | async-start | bytes 25165824 | tf_op jit(solution)/shard_map/all_gather | solution.py:106
  7.3 150.7 %all-gather.10.cloned.1.call-start = ((), (), s32[]{:S(2)}) async-start(), calls=%async_computation.3 | async-start | bytes 5505024 | tf_op jit(solution)/shard_map/all_gather | solution.py:108
  8.0 153.3 %all-gather.8.cloned.1.call-start = ((), (), s32[]{:S(2)}) async-start(), calls=%async_computation.2 | async-start | bytes 5505024 | tf_op jit(solution)/shard_map/all_gather | solution.py:109
  8.7 1.2 copy-start.2
  8.8 1.4 copy-start.17
  8.8 169.3 %all-gather.12.cloned.1.call-start = ((), (), s32[]{:S(2)}) async-start(), calls=%async_computation.4 | async-start | bytes 25165824 | tf_op jit(solution)/shard_map/all_gather | solution.py:110
  14.3 2.6 copy-start.16
  14.4 4.1 %collective-permute-start = (f32[512,896]{1,0:T(8,128)}, f32[512,896]{1,0:T(8,128)}, u32[]{:S(2)}, u32[]{:S(2)}) collective-permute-start(f32[512,896]{1,0:T(8,128)} %fusion.101), channel_id=1, source_target_pairs={{0,2},{2,0},{1,3},{3,1},{4,6},{6,4},{5,7},{7,5},{8,10},{10,8},{9,1... | collective-permute-start | bytes 5505032 | tf_op jit(solution)/shard_map/ppermute | solution.py:28
  15.7 5.9 %copy-start.4 = (bf16[256,2048]{1,0:T(8,128)(2,1)}, bf16[256,2048]{1,0:T(8,128)(2,1)S(1)}, u32[]{:S(2)}) copy-start(bf16[256,2048]{1,0:T(8,128)(2,1)S(1)} %constant_dynamic-slice_fusion) | copy-start | bytes 3145732
  15.7 36.7 %collective-permute-start.3 = (bf16[256,2048]{1,0:T(8,128)(2,1)S(1)}, bf16[256,2048]{1,0:T(8,128)(2,1)}, u32[]{:S(2)}, u32[]{:S(2)}) collective-permute-start(bf16[256,2048]{1,0:T(8,128)(2,1)S(1)} %constant_dynamic-slice_fusion), channel_id=1, source_target_pairs={{0,1},{1,0},{2,3},{3,2},{4,5},{5,4},{6,7},{7,6},{8,9},{9,8},{10,11... | collective-permute-start | bytes 3145736 | tf_op jit(solution)/shard_map/ppermute | solution.py:28
  21.6 1.4 copy-start.8
  23.0 28.1 %collective-permute-start.1 = (f32[4,1,32,896]{3,2,0,1:T(8,128)S(1)}, f32[4,1,32,896]{3,2,0,1:T(8,128)S(1)}, u32[]{:S(2)}, u32[]{:S(2)}) collective-permute-start(f32[4,1,32,896]{3,2,0,1:T(8,128)S(1)} %dynamic-slice_bitcast_fusion), channel_id=1, source_target_pairs={{0,1},{1,0},{2,3},{3,2},{4,5},{5,4},{6,7},{7,6},{8,9},{9,8},{10,11... | collective-permute-start | bytes 1376264 | tf_op jit(solution)/shard_map/ppermute | solution.py:28
  24.8 27.5 %copy-start.5 = (bf16[256,2048]{1,0:T(8,128)(2,1)S(1)}, bf16[256,2048]{1,0:T(8,128)(2,1)}, u32[]{:S(2)}) copy-start(bf16[256,2048]{1,0:T(8,128)(2,1)} %copy-done.4) | copy-start | bytes 3145732
  52.2 2.5 copy-start.3
  52.2 2.5 collective-permute-start.2
  57.8 11.2 %copy-start.14 = (f32[1,4096]{1,0:T(1,128)S(1)}, f32[1,4096]{1,0:T(1,128)}, u32[]{:S(2)}) copy-start(f32[1,4096]{1,0:T(1,128)} %param.17) | copy-start | bytes 49156
  57.8 61.3 %all-to-all-start = ((bf16[32,64,896]{2,1,0:T(8,128)(2,1)}), bf16[32,64,896]{2,1,0:T(8,128)(2,1)}, u32[]{:S(2)}, u32[]{:S(2)}) async-start(bf16[32,64,896]{2,1,0:T(8,128)(2,1)} %gather_fusion), calls=%async_computation | async-start | bytes 7340032 | tf_op jit(solution)/shard_map/all_to_all | solution.py:144
  121.8 23.1 %collective-permute-start.4 = (bf16[8,64,896]{2,1,0:T(8,128)(2,1)S(1)}, bf16[8,64,896]{2,1,0:T(8,128)(2,1)S(1)}, u32[]{:S(2)}, u32[]{:S(2)}) collective-permute-start(bf16[8,64,896]{2,1,0:T(8,128)(2,1)S(1)} %gather_fusion.1), channel_id=1, source_target_pairs={{0,1},{1,0},{2,3},{3,2},{4,5},{5,4},{6,7},{7,6},{8,9},{9,8},{10,11... | collective-permute-start | bytes 2752520 | tf_op jit(solution)/shard_map/ppermute | solution.py:28
  145.7 4.3 %collective-permute-start.5 = (bf16[8,128,896]{2,1,0:T(8,128)(2,1)S(1)}, bf16[8,128,896]{2,1,0:T(8,128)(2,1)}, u32[]{:S(2)}, u32[]{:S(2)}) collective-permute-start(bf16[8,128,896]{2,1,0:T(8,128)(2,1)S(1)} %maximum_select_fusion.2), channel_id=1, source_target_pairs={{0,2},{2,0},{1,3},{3,1},{4,6},{6,4},{5,7},{7,5},{8,10},{10,8},{9,1... | collective-permute-start | bytes 5505032 | tf_op jit(solution)/shard_map/ppermute | solution.py:28
  161.0 1.2 copy-start.12
  167.1 3.4 %copy-start.10 = (bf16[4,128,896]{2,1,0:T(8,128)(2,1)S(1)}, bf16[4,128,896]{2,1,0:T(8,128)(2,1)}, u32[]{:S(2)}) copy-start(bf16[4,128,896]{2,1,0:T(8,128)(2,1)} %get-tuple-element.17) | copy-start | bytes 2752516
  170.4 3.2 %copy-start.19 = (bf16[2,896,1024]{2,1,0:T(8,128)(2,1)S(1)}, bf16[2,896,1024]{2,1,0:T(8,128)(2,1)}, u32[]{:S(2)}) copy-start(bf16[2,896,1024]{2,1,0:T(8,128)(2,1)} %all-gather.8.cloned.1.call-done) | copy-start | bytes 11010052
  182.8 23.2 %collective-permute-start.6 = (bf16[128,2048]{1,0:T(8,128)(2,1)S(1)}, bf16[128,2048]{1,0:T(8,128)(2,1)S(1)}, u32[]{:S(2)}, u32[]{:S(2)}) collective-permute-start(bf16[128,2048]{1,0:T(8,128)(2,1)S(1)} %dynamic-slice_convert_fusion.3), channel_id=1, source_target_pairs={{0,1},{1,0},{2,3},{3,2},{4,5},{5,4},{6,7},{7,6},{8,9},{9,8},{10,11... | collective-permute-start | bytes 1572872 | tf_op jit(solution)/shard_map/ppermute | solution.py:28
  184.6 16.8 %copy-start.13 = (bf16[4,128,896]{2,1,0:T(8,128)(2,1)S(1)}, bf16[4,128,896]{2,1,0:T(8,128)(2,1)}, u32[]{:S(2)}) copy-start(bf16[4,128,896]{2,1,0:T(8,128)(2,1)} %get-tuple-element.18) | copy-start | bytes 2752516
  184.6 16.8 %copy-start.18 = (bf16[2,896,1024]{2,1,0:T(8,128)(2,1)S(1)}, bf16[2,896,1024]{2,1,0:T(8,128)(2,1)}, u32[]{:S(2)}) copy-start(bf16[2,896,1024]{2,1,0:T(8,128)(2,1)} %all-gather.10.cloned.1.call-done) | copy-start | bytes 11010052
  189.5 25.3 %collective-permute-start.9 = (bf16[128,2048]{1,0:T(8,128)(2,1)S(1)}, bf16[128,2048]{1,0:T(8,128)(2,1)S(1)}, u32[]{:S(2)}, u32[]{:S(2)}) collective-permute-start(bf16[128,2048]{1,0:T(8,128)(2,1)S(1)} %dynamic-slice_convert_fusion.1), channel_id=1, source_target_pairs={{0,1},{1,0},{2,3},{3,2},{4,5},{5,4},{6,7},{7,6},{8,9},{9,8},{10,11... | collective-permute-start | bytes 1572872 | tf_op jit(solution)/shard_map/ppermute | solution.py:28
  201.5 2.0 copy-start.20
  201.5 29.2 %slice-start = ((s8[16777216]{0:T(1024)(128)(4,1)}), s8[4194304]{0:T(1024)(128)(4,1)S(1)}, s32[]{:S(2)}) async-start(s8[16777216]{0:T(1024)(128)(4,1)} %bitcast.234), calls=%async_computation.5 | async-start | bytes 8388608
  203.5 27.2 %slice-start.1 = ((s8[16777216]{0:T(1024)(128)(4,1)}), s8[4194304]{0:T(1024)(128)(4,1)S(1)}, s32[]{:S(2)}) async-start(s8[16777216]{0:T(1024)(128)(4,1)} %bitcast.234), calls=%async_computation.6 | async-start | bytes 8388608
  204.8 10.1 %copy-start.9 = (bf16[512,2048]{1,0:T(8,128)(2,1)S(1)}, bf16[512,2048]{1,0:T(8,128)(2,1)}, u32[]{:S(2)}) copy-start(bf16[512,2048]{1,0:T(8,128)(2,1)} %param.11) | copy-start | bytes 6291460
  206.0 9.7 %copy-start.11 = (bf16[4,128,896]{2,1,0:T(8,128)(2,1)S(1)}, bf16[4,128,896]{2,1,0:T(8,128)(2,1)}, u32[]{:S(2)}) copy-start(bf16[4,128,896]{2,1,0:T(8,128)(2,1)} %get-tuple-element.17) | copy-start | bytes 2752516
  206.0 24.7 %slice-start.2 = ((s8[16777216]{0:T(1024)(128)(4,1)}), s8[4194304]{0:T(1024)(128)(4,1)S(1)}, s32[]{:S(2)}) async-start(s8[16777216]{0:T(1024)(128)(4,1)} %bitcast.234), calls=%async_computation.7 | async-start | bytes 8388608
  215.4 14.9 %collective-permute-start.7 = (bf16[128,2048]{1,0:T(8,128)(2,1)S(1)}, bf16[128,2048]{1,0:T(8,128)(2,1)S(1)}, u32[]{:S(2)}, u32[]{:S(2)}) collective-permute-start(bf16[128,2048]{1,0:T(8,128)(2,1)S(1)} %get-tuple-element.15), channel_id=1, source_target_pairs={{0,1},{1,0},{2,3},{3,2},{4,5},{5,4},{6,7},{7,6},{8,9},{9,8},{10,11... | collective-permute-start | bytes 1572872 | tf_op jit(solution)/shard_map/ppermute | solution.py:28
  217.0 13.7 %slice-start.3 = ((s8[16777216]{0:T(1024)(128)(4,1)}), s8[4194304]{0:T(1024)(128)(4,1)S(1)}, s32[]{:S(2)}) async-start(s8[16777216]{0:T(1024)(128)(4,1)} %bitcast.234), calls=%async_computation.8 | async-start | bytes 8388608
  218.6 12.1 %copy-start.15 = (f32[1,1,4096]{2,1,0:T(1,128)S(1)}, f32[1,1,4096]{2,1,0:T(1,128)}, u32[]{:S(2)}) copy-start(f32[1,1,4096]{2,1,0:T(1,128)} %get-tuple-element.21) | copy-start | bytes 49156
  219.9 19.6 %collective-permute-start.10 = (bf16[128,2048]{1,0:T(8,128)(2,1)S(1)}, bf16[128,2048]{1,0:T(8,128)(2,1)S(1)}, u32[]{:S(2)}, u32[]{:S(2)}) collective-permute-start(bf16[128,2048]{1,0:T(8,128)(2,1)S(1)} %get-tuple-element.16), channel_id=1, source_target_pairs={{0,1},{1,0},{2,3},{3,2},{4,5},{5,4},{6,7},{7,6},{8,9},{9,8},{10,11... | collective-permute-start | bytes 1572872 | tf_op jit(solution)/shard_map/ppermute | solution.py:28
  233.3 1.0 copy-start.6
  245.6 1.0 copy-start.7
  255.6 14.9 %collective-permute-start.11 = (bf16[128,2048]{1,0:T(8,128)(2,1)S(1)}, bf16[128,2048]{1,0:T(8,128)(2,1)S(1)}, u32[]{:S(2)}, u32[]{:S(2)}) collective-permute-start(bf16[128,2048]{1,0:T(8,128)(2,1)S(1)} %dynamic-slice_convert_fusion), channel_id=1, source_target_pairs={{0,1},{1,0},{2,3},{3,2},{4,5},{5,4},{6,7},{7,6},{8,9},{9,8},{10,11... | collective-permute-start | bytes 1572872 | tf_op jit(solution)/shard_map/ppermute | solution.py:28
  260.7 18.2 %collective-permute-start.8 = (bf16[128,2048]{1,0:T(8,128)(2,1)S(1)}, bf16[128,2048]{1,0:T(8,128)(2,1)S(1)}, u32[]{:S(2)}, u32[]{:S(2)}) collective-permute-start(bf16[128,2048]{1,0:T(8,128)(2,1)S(1)} %dynamic-slice_convert_fusion.2), channel_id=1, source_target_pairs={{0,1},{1,0},{2,3},{3,2},{4,5},{5,4},{6,7},{7,6},{8,9},{9,8},{10,11... | collective-permute-start | bytes 1572872 | tf_op jit(solution)/shard_map/ppermute | solution.py:28
  270.5 9.7 %copy-start.1 = (bf16[512,896]{1,0:T(8,128)(2,1)S(1)}, bf16[512,896]{1,0:T(8,128)(2,1)}, u32[]{:S(2)}) copy-start(bf16[512,896]{1,0:T(8,128)(2,1)} %param.16) | copy-start | bytes 2752516
Sparse Core Ops, SparseCore 0:
  9.0 34.5 all-gather.5
  45.2 16.9 all-gather.9
  63.9 16.9 all-gather.7
  82.3 34.0 all-gather.11
